TPU v7x, 128 devices: a whole 4x4x4 slice. The times are simulated.
128 devices in a mesh: seq: 32 (over y, z, core), tp: 4 (over x).
Axes of the slice: x: 4, y: 4, z: 4, core: 2. Of those that a mesh axis runs over, the one named last changes fastest.
Arguments:
- rollout_rows: bfloat16 [16384, 8192], P('seq', 'tp'), may hold values from -100 to 100
- plan: int32 [16384], P('seq'), may hold values from 0 to 16383, as said below
- segment_ids: int32 [16384], P('seq'), may hold values from 0 to 256, as said below
- norm_gain: float32 [8192], replicated, may hold values from 0.1 to 1.9
- q_weight: bfloat16 [8192, 4096], P('seq', 'tp'), may hold values from -0.0625 to 0.0625
- k_weight: bfloat16 [8192, 512], P('seq', 'tp'), may hold values from -0.0625 to 0.0625
- v_weight: bfloat16 [8192, 512], P('seq', 'tp'), may hold values from -0.0625 to 0.0625
- q_bias: float32 [4096], P('tp'), may hold values from -40 to 40
- k_bias: float32 [512], P('tp'), may hold values from -40 to 40
- v_bias: float32 [512], P('tp'), may hold values from -3 to 3
Outputs:
- context: bfloat16 [16384, 4096], P('seq', 'tp')
Inputs may be any that keep to these rules, and one draw needn't show every extreme that they name: plan is a permutation of the learner rows; rollout row r goes to learner shard plan[r] // 512. The rows of one device go 16 to every learner shard, except 20 rows to one shard and 12 rows to another. `segment_ids`: within each learner shard the ids start at 0, never fall and rise by one at each new sequence; each sequence has 1 to 256 rows and one sequence of every shard has exactly 256; no sequence crosses a shard.
All inputs are finite; a program needn't handle non-finite values.
Results may differ from a plain program's by a relative error of at most 0.012.
The roundings to bfloat16 on the way count: a program that leaves them out, or rounds other values in their place, can miss the bound.
Values may be sent and summed in bfloat16 or wider, within the bound.
No kernel may reach another device: no remote copies, remote signals or barrier semaphores. Data moves between devices by JAX's collectives and lax.ppermute only.
A program may use at most 128 MiB of HBM per device.

v0:
```python
import math

import jax
import jax.numpy as jnp
from jax import lax
from jax.sharding import Mesh
from jax.sharding import PartitionSpec as P


HEAD = 128


EPS = 1e-06
ROPE_BASE = 1000000.0

CHIPS = "chips"
CORE = "core"
SEQ = (CHIPS, CORE)
TP = "tp"


def rotate(tensor, positions):
    half_size = tensor.shape[-1] // 2
    frequency = jnp.exp(
        jnp.arange(half_size, dtype=jnp.float32) * (-2.0 * math.log(ROPE_BASE) / tensor.shape[-1])
    )
    angles = positions.astype(jnp.float32)[:, None] * frequency[None, :]
    cosine = jnp.cos(angles)[:, None, :]
    sine_part = jnp.sin(angles)[:, None, :]
    front_half = tensor[..., :half_size]
    back_half = tensor[..., half_size:]
    return jnp.concatenate(
        [front_half * cosine - back_half * sine_part, back_half * cosine + front_half * sine_part],
        axis=-1,
    )


def positions_of(segments):
    length = segments.shape[-1]
    counter = jnp.arange(length, dtype=jnp.int32)
    starts = jnp.concatenate([jnp.ones((1,), dtype=bool), segments[1:] != segments[:-1]])
    marked = jnp.where(starts, counter, jnp.zeros_like(counter))
    return counter - lax.cummax(marked, axis=0)


def make_local(chip_count, core_count, tp_count):
    peer_count = chip_count * core_count

    def body(
        rollout_rows, plan, segment_ids, norm_gain, q_weight, k_weight, v_weight, q_bias, k_bias, v_bias
    ):
        row_count, width = rollout_rows.shape
        slots_each = row_count // peer_count + row_count // (4 * peer_count)
        q_cols = q_weight.shape[1]
        k_cols = k_weight.shape[1]


        weights = jnp.concatenate([q_weight, k_weight, v_weight], axis=1)
        own_weights = lax.all_gather(weights, CHIPS, axis=0, tiled=False)
        other_weights = lax.ppermute(
            own_weights, CORE, [(c, (c + 1) % core_count) for c in range(core_count)]
        )

        target = plan // row_count
        learner_slot = plan % row_count
        matches = (target[:, None] == jnp.arange(peer_count, dtype=jnp.int32)[None, :]).astype(
            jnp.int32
        )
        ranking = jnp.sum((jnp.cumsum(matches, axis=0) - 1) * matches, axis=1)
        slot_hits = (target[None, None, :] == jnp.arange(peer_count, dtype=jnp.int32)[:, None, None]) & (
            ranking[None, None, :] == jnp.arange(slots_each, dtype=jnp.int32)[None, :, None]
        )
        tagged = jnp.sum(jnp.where(slot_hits, learner_slot[None, None, :] + 1, 0), axis=2)
        tag_row = jnp.concatenate(
            [
                (tagged // 32).astype(jnp.bfloat16),
                (tagged % 32).astype(jnp.bfloat16),
                jnp.zeros((peer_count, width - 2 * slots_each), jnp.bfloat16),
            ],
            axis=1,
        )
        picked = jnp.einsum(
            "psr,rf->psf",
            slot_hits.astype(jnp.bfloat16),
            rollout_rows,
            preferred_element_type=jnp.float32,
        ).astype(jnp.bfloat16)
        payload = jnp.concatenate([picked, tag_row[:, None, :]], axis=1)
        arrived = lax.all_to_all(payload, SEQ, split_axis=0, concat_axis=0, tiled=True)
        tags = arrived[:, slots_each, : 2 * slots_each].astype(jnp.int32)
        labels = tags[:, :slots_each] * 32 + tags[:, slots_each:] - 1
        row_numbers = jnp.arange(row_count, dtype=jnp.int32)
        label_hits = labels[None, :, :] == row_numbers[:, None, None]
        learner_part = jnp.einsum(
            "rps,psf->rf",
            label_hits.astype(jnp.bfloat16),
            arrived[:, :slots_each, :],
            preferred_element_type=jnp.float32,
        ).astype(jnp.bfloat16)

        tp_index = lax.axis_index(TP)
        core_index = lax.axis_index(CORE)
        wide = learner_part.astype(jnp.float32)
        own_sq = jnp.sum(wide * wide, axis=-1)
        others = [
            lax.ppermute(own_sq, TP, [(t, (t + k) % tp_count) for t in range(tp_count)])
            for k in range(1, tp_count)
        ]
        total_sq = own_sq
        for other in others:
            total_sq = total_sq + other
        scale = lax.rsqrt(total_sq / (width * tp_count) + EPS)[:, None]

        to_right = [(t, (t + 1) % tp_count) for t in range(tp_count)]
        to_left = [(t, (t - 1) % tp_count) for t in range(tp_count)]
        half = width // 2
        from_left = lax.ppermute(learner_part, TP, to_right)
        from_right = lax.ppermute(learner_part, TP, to_left)
        far_a = lax.ppermute(from_left[:, :half], TP, to_right)
        far_b = lax.ppermute(from_right[:, half:], TP, to_left)
        far = jnp.concatenate([far_a, far_b], axis=1)
        pieces = [learner_part, from_left, far, from_right]

        block = width // (4 * core_count)
        span = 4 * block
        own_rows = own_weights.reshape(tp_count, span, own_weights.shape[-1])
        other_rows = other_weights.reshape(tp_count, span, own_weights.shape[-1])

        def core_block(x, c):
            return jnp.concatenate(
                [x[:, (hl * core_count + c) * block : (hl * core_count + c + 1) * block] for hl in range(4)],
                axis=1,
            )

        def normalize(piece, k, scale, norm_gain, tp_index):
            quarter = (tp_index - k) % tp_count
            gain = lax.dynamic_slice_in_dim(norm_gain, quarter * width, width)
            return (piece.astype(jnp.float32) * scale * gain).astype(jnp.bfloat16)

        def project(normed, k, tp_index, core_index):
            quarter = (tp_index - k) % tp_count
            first = core_block(normed, 0)
            second = core_block(normed, 1)
            mine = jnp.where(core_index == 0, first, second)
            theirs = jnp.where(core_index == 0, second, first)
            total = None
            for cols, rows_of in ((mine, own_rows), (theirs, other_rows)):
                rows = lax.dynamic_index_in_dim(rows_of, quarter, axis=0, keepdims=False)
                part = jnp.dot(cols, rows, preferred_element_type=jnp.float32)
                total = part if total is None else total + part
            return total

        projected = None
        for k in (0, 1, 3):
            normed = normalize(pieces[k], k, scale, norm_gain, tp_index)
            part = project(normed, k, tp_index, core_index)
            projected = part if projected is None else projected + part
        projected = lax.optimization_barrier(projected)
        far_piece, far_scale, far_gain, far_tp, far_core = lax.optimization_barrier(
            (pieces[2], scale, norm_gain, tp_index, core_index)
        )
        normed = normalize(far_piece, 2, far_scale, far_gain, far_tp)
        projected = projected + project(normed, 2, far_tp, far_core)
        queries = projected[:, :q_cols]
        key_proj = projected[:, q_cols : q_cols + k_cols]
        value_proj = projected[:, q_cols + k_cols :]
        local_heads = q_cols // HEAD
        local_groups = k_cols // HEAD
        group_size = local_heads // local_groups
        positions = positions_of(segment_ids)
        q_rot = rotate((queries + q_bias).reshape(row_count, local_heads, HEAD), positions).astype(
            jnp.bfloat16
        )
        q_rot = q_rot.reshape(row_count, local_groups, group_size, HEAD)
        k_rot = rotate((key_proj + k_bias).reshape(row_count, local_groups, HEAD), positions).astype(
            jnp.bfloat16
        )
        value_heads = (value_proj + v_bias).astype(jnp.bfloat16).reshape(row_count, local_groups, HEAD)
        block_rows = min(512, row_count)
        row_index = jnp.arange(row_count, dtype=jnp.int32)
        scores = jnp.einsum(
            "qkgd,pkd->kgqp", q_rot, k_rot, preferred_element_type=jnp.float32
        ) / math.sqrt(HEAD)
        allowed = (segment_ids[0:block_rows, None] == segment_ids[None, :block_rows]) & (
            row_index[0:block_rows, None] >= row_index[None, :block_rows]
        )
        scores = jnp.where(allowed[None, None], scores, -jnp.inf)
        highest = jnp.max(scores, axis=-1, keepdims=True)
        expo = jnp.exp(scores - highest)
        probs = (expo / jnp.sum(expo, axis=-1, keepdims=True)).astype(jnp.bfloat16)
        mixed = jnp.einsum("kgqp,pkd->qkgd", probs, value_heads, preferred_element_type=jnp.float32)
        outputs = mixed.astype(jnp.bfloat16).reshape(block_rows, local_heads * HEAD)
        return outputs

    return body


def solution(mesh):
    seq_count, tp_count = mesh.devices.shape
    core_count = 2
    chip_count = seq_count // core_count
    split = Mesh(mesh.devices.reshape(chip_count, core_count, tp_count), (CHIPS, CORE, TP))
    in_specs = (
        P(SEQ, TP),
        P(SEQ),
        P(SEQ),
        P(),
        P(SEQ, TP),
        P(SEQ, TP),
        P(SEQ, TP),
        P(TP),
        P(TP),
        P(TP),
    )
    out_specs = P(SEQ, TP)
    return jax.shard_map(
        make_local(chip_count, core_count, tp_count),
        mesh=split,
        in_specs=in_specs,
        out_specs=out_specs,
        check_vma=False,
    )
```

profile of v0, /device:TPU:0, one launch (start us, length us, event | category | flops | bytes accessed | tf_op | source)
XLA Modules:
  0.0 271.5 jit_solution(12969515295223595778)
XLA Ops:
  6.5 2.1 pad_maximum_fusion.10
  8.7 0.7 add_select_fusion.3
  9.4 1.2 reduce-window.15
  10.6 0.2 slice_reduce_fusion
  10.8 0.1 fusion.81
  11.0 0.4 fusion.38
  11.4 0.1 copy.25
  11.6 0.2 concatenate.58
  11.7 3.0 %convolution_convert_fusion = bf16[32,20,2048]{2,0,1:T(8,128)(2,1)} fusion(bf16[512,2048]{1,0:T(8,128)(2,1)S(1)} %copy-done, pred[20,512]{1,0:T(8,128)(4,1)S(1)} %iota_compare_fusion.6, pred[32,512]{1,0:T(8,128)(4,1)S(1)} %iota_compare_fusion.5), kind=kOutput, calls=%fused_computation.24 | convolution fusion | flops 1343815680 | bytes 4745216 | tf_op jit(solution)/shard_map/psr,rf->psf/dot_general | solution.py:82
  14.8 77.7 %all-gather.3.cloned.1.call-done = bf16[4096,1280]{1,0:T(8,128)(2,1)} async-done(((bf16[256,1280]{1,0:T(8,128)(2,1)}), bf16[4096,1280]{1,0:T(8,128)(2,1)}) %all-gather.3.cloned.1.call-update) | async-done | bytes 10485776 | tf_op jit(solution)/shard_map/all_gather | solution.py:59
  92.5 2.0 pad_maximum_fusion
  94.5 1.5 copy.29
  96.0 44.7 %all_to_all.5 = bf16[32,21,2048]{2,1,0:T(8,128)(2,1)S(1)} all-to-all(bf16[32,21,2048]{2,1,0:T(8,128)(2,1)S(1)} %copy.29), channel_id=1, replica_groups=mesh['chips'=16,'core'=2,'tp'=4] {'chips','core'}, dimensions={0} | all-to-all | bytes 5505024 | tf_op jit(solution)/shard_map/all_to_all | solution.py:89
  140.9 0.1 copy.31
  140.9 4.0 %fusion.2 = (f32[512]{0:T(512)S(1)}, bf16[512,2048]{1,0:T(8,128)(2,1)}) fusion(bf16[32,20,2048]{2,1,0:T(8,128)(2,1)S(1)} %bitcast.108, s32[32,20]{0,1:T(8,128)S(1)} %copy.31), kind=kOutput, calls=%fused_computation.7 | convolution fusion | flops 1346698752 | bytes 4723200 | tf_op jit(solution)/shard_map/rps,psf->rf/dot_general | solution.py:94
  145.0 2.7 collective-permute-start.5
  147.8 0.1 add_select_fusion.4
  147.8 0.3 reduce-window.19
  148.3 0.1 slice_reduce_fusion.1
  148.4 0.1 fusion.90
  148.5 0.2 fusion.51
  148.7 1.0 multiply_cosine_fusion
  149.7 3.3 %collective-permute-start.2 = (f32[512]{0:T(512)S(1)}, f32[512]{0:T(512)S(1)}, u32[]{:S(2)}, u32[]{:S(2)}) collective-permute-start(f32[512]{0:T(512)S(1)} %get-tuple-element.65), channel_id=1, source_target_pairs={{0,3},{1,0},{2,1},{3,2},{4,7},{5,4},{6,5},{7,6},{8,11},{9,8},{10,9... | collective-permute-start | bytes 6152 | tf_op jit(solution)/shard_map/ppermute | solution.py:106
  153.0 40.6 %collective-permute-done.2 = f32[512]{0:T(512)S(1)} collective-permute-done((f32[512]{0:T(512)S(1)}, f32[512]{0:T(512)S(1)}, u32[]{:S(2)}, u32[]{:S(2)}) %collective-permute-start.2) | collective-permute-done | bytes 2080 | tf_op jit(solution)/shard_map/ppermute | solution.py:106
  193.5 1.1 collective-permute-start
  194.6 1.3 collective-permute-done.1
  196.0 2.7 collective-permute-done
  198.7 0.1 slice.235
  198.8 2.1 collective-permute-start.7
  200.9 1.3 slice.234
  202.2 0.3 collective-permute-start.6
  202.4 4.7 %fusion.4 = (bf16[512,2048]{1,0:T(8,128)(2,1)S(1)}, bf16[512,2048]{1,0:T(8,128)(2,1)S(1)}, bf16[512,2048]{1,0:T(8,128)(2,1)S(1)}) fusion(bf16[512,2048]{1,0:T(8,128)(2,1)} %get-tuple-element.66, f32[2048]{0:T(1024)S(1)} %get-tuple-element.53, f32[512]{0:T(512)S(1)} %add_rsqrt_fusion, f32[2048]{0:T(1024)S(1)} %get-tuple-element.54, ...), kind=kLoop, calls=%fused_computation.9 | loop fusion | flops 12582912 | bytes 12609536 | tf_op jit(solution)/shard_map/convert_element_type | solution.py:138
  207.1 1.3 fusion.115
  208.5 1.9 fusion.113
  210.4 12.2 %collective-permute-done.7 = bf16[512,1024]{1,0:T(8,128)(2,1)S(1)} collective-permute-done((bf16[512,1024]{1,0:T(8,128)(2,1)S(1)}, bf16[512,1024]{1,0:T(8,128)(2,1)S(1)}, u32[]{:S(2)}, u32[]{:S(2)}) %collective-permute-start.7) | collective-permute-done | bytes 1048608 | tf_op jit(solution)/shard_map/ppermute | solution.py:120
  222.6 4.2 %collective-permute-done.6 = bf16[512,1024]{1,0:T(8,128)(2,1)S(1)} collective-permute-done((bf16[512,1024]{1,0:T(8,128)(2,1)S(1)}, bf16[512,1024]{1,0:T(8,128)(2,1)S(1)}, u32[]{:S(2)}, u32[]{:S(2)}) %collective-permute-start.6) | collective-permute-done | bytes 1048608 | tf_op jit(solution)/shard_map/ppermute | solution.py:119
  226.8 0.2 pad_maximum_fusion.1
  227.1 0.5 multiply_convert_fusion
  227.7 0.1 fusion.112
  227.8 0.7 copy-done.8
  228.6 0.1 copy-done.9
  228.6 0.1 copy-done.10
  228.7 0.1 copy-done.11
  228.8 0.1 copy-done.12
  228.9 0.1 copy-done.13
  229.0 0.1 copy-done.14
  229.0 0.1 copy-done.15
  229.2 3.4 %fusion.16 = f32[512,1280]{1,0:T(8,128)S(1)} fusion(bf16[4,1024,1280]{2,1,0:T(8,128)(2,1)} %bitcast.113, s32[]{:T(128)S(6)} %select_n.147, pred[]{:T(512)S(6)} %eq.114, bf16[512,256]{1,0:T(8,128)(2,1)S(1)} %copy-done.9, bf16[512,256]{1,0:T(8,128)(2,1)S(1)} %copy-done.10, bf16[512,256]{1,0:T(8,128)(2,1)S(1)} %copy-done.11, ...), kind=kOutput, calls=%fused_computation.31 | convolution fusion | flops 1351090176 | bytes 7340037 | tf_op jit(solution)/shard_map/dot_general | solution.py:149
  232.8 3.5 %fusion.19 = f32[512,1280]{1,0:T(8,128)S(1)} fusion(bf16[4,1024,1280]{2,1,0:T(8,128)(2,1)} %bitcast.114, s32[]{:T(128)S(6)} %select_n.142, pred[]{:T(512)S(6)} %eq.114, bf16[512,256]{1,0:T(8,128)(2,1)S(1)} %copy-done.22, bf16[512,256]{1,0:T(8,128)(2,1)S(1)} %copy-done.21, bf16[512,256]{1,0:T(8,128)(2,1)S(1)} %copy-done.20, ...), kind=kOutput, calls=%fused_computation.34 | convolution fusion | flops 1351090176 | bytes 7340037 | tf_op jit(solution)/shard_map/dot_general | solution.py:149
  236.4 1.6 fusion.22
  238.0 1.6 fusion.13
  239.6 3.3 %convolution_add_fusion.1 = f32[512,1280]{1,0:T(8,128)S(1)} fusion(f32[512,1280]{1,0:T(8,128)S(1)} %fusion.16, bf16[4,1024,1280]{2,1,0:T(8,128)(2,1)} %bitcast.10, s32[]{:T(128)S(6)} %select_n.147, pred[]{:T(512)S(6)} %eq.114, bf16[512,256]{1,0:T(8,128)(2,1)S(1)} %copy-done.9, bf16[512,256]{1,0:T(8,128)(2,1)S(1)} %copy-done.10, ...), kind=kOutput, calls=%fused_computation.18 | convolution fusion | flops 1351745536 | bytes 9961477 | tf_op jit(solution)/shard_map/dot_general | solution.py:149
  242.9 3.3 %convolution_add_fusion.2 = f32[512,1280]{1,0:T(8,128)S(1)} fusion(f32[512,1280]{1,0:T(8,128)S(1)} %fusion.19, bf16[4,1024,1280]{2,1,0:T(8,128)(2,1)} %bitcast.10, s32[]{:T(128)S(6)} %select_n.142, pred[]{:T(512)S(6)} %eq.114, bf16[512,256]{1,0:T(8,128)(2,1)S(1)} %copy-done.22, bf16[512,256]{1,0:T(8,128)(2,1)S(1)} %copy-done.21, ...), kind=kOutput, calls=%fused_computation.19 | convolution fusion | flops 1351745536 | bytes 9961477 | tf_op jit(solution)/shard_map/dot_general | solution.py:149
  246.2 3.6 %fusion.10 = f32[512,1280]{1,0:T(8,128)S(1)} fusion(f32[512,1280]{1,0:T(8,128)S(1)} %convolution_add_fusion.1, f32[512,1280]{1,0:T(8,128)S(1)} %convolution_add_fusion.2, f32[512,1280]{1,0:T(8,128)S(1)} %fusion.22, bf16[4,1024,1280]{2,1,0:T(8,128)(2,1)} %bitcast.10, s32[]{:T(128)S(6)} %select_n.137, pred[]{:T(512)S(6)} %eq.114, ...), kind=kOutput, calls=%fused_computation.23 | convolution fusion | flops 1353056256 | bytes 15204357 | tf_op jit(solution)/shard_map/dot_general | solution.py:149
  249.8 3.3 %fusion.9 = f32[512,1280]{1,0:T(8,128)S(1)} fusion(f32[512,1280]{1,0:T(8,128)S(1)} %fusion.10, f32[512,1280]{1,0:T(8,128)S(1)} %fusion.13, bf16[4,1024,1280]{2,1,0:T(8,128)(2,1)} %bitcast.10, s32[]{:T(128)S(6)} %select_n.153, pred[]{:T(512)S(6)} %eq.131, bf16[512,256]{1,0:T(8,128)(2,1)S(1)} %get-tuple-element.20, ...), kind=kOutput, calls=%fused_computation.22 | convolution fusion | flops 1352400896 | bytes 12582917 | tf_op jit(solution)/shard_map/dot_general | solution.py:149
  253.1 0.3 fusion.32
  253.4 0.5 copy.46
  253.9 0.7 fusion.111
  254.6 1.2 fusion.79
  255.9 0.8 subtract_convert_fusion
  256.7 2.2 fusion.1
  258.9 1.7 fusion
  260.7 2.7 fusion.35
  263.3 1.3 copy.37
  (83 shorter events, 0.6 us)
Async XLA Ops:
  6.5 5.2 %copy-start = (bf16[512,2048]{1,0:T(8,128)(2,1)S(1)}, bf16[512,2048]{1,0:T(8,128)(2,1)}, u32[]{:S(2)}) copy-start(bf16[512,2048]{1,0:T(8,128)(2,1)} %param.10) | copy-start | bytes 6291460
  6.5 85.9 %all-gather.3.cloned.1.call-start = ((), (), s32[]{:S(2)}) async-start(), calls=%async_computation.1 | async-start | bytes 11141120 | tf_op jit(solution)/shard_map/all_gather | solution.py:59
  92.5 147.1 %collective-permute-start.3 = (bf16[16,256,1280]{2,1,0:T(8,128)(2,1)}, bf16[16,256,1280]{2,1,0:T(8,128)(2,1)}, u32[]{:S(2)}, u32[]{:S(2)}) collective-permute-start(bf16[16,256,1280]{2,1,0:T(8,128)(2,1)} %bitcast.112), channel_id=1, source_target_pairs={{0,4},{4,0},{1,5},{5,1},{2,6},{6,2},{3,7},{7,3},{8,12},{12,8},{9,1... | collective-permute-start | bytes 31457288 | tf_op jit(solution)/shard_map/ppermute | solution.py:60
  140.9 6.7 %copy-start.24 = (s32[512]{0:T(512)S(1)}, s32[512]{0:T(512)}, u32[]{:S(2)}) copy-start(s32[512]{0:T(512)} %param.12) | copy-start | bytes 6148
  140.9 53.7 %copy-start.25 = (f32[8192]{0:T(1024)S(1)}, f32[8192]{0:T(1024)}, u32[]{:S(2)}) copy-start(f32[8192]{0:T(1024)} %param.13) | copy-start | bytes 98308
  145.0 53.7 %collective-permute-start.5 = (bf16[512,2048]{1,0:T(8,128)(2,1)}, bf16[512,2048]{1,0:T(8,128)(2,1)S(1)}, u32[]{:S(2)}, u32[]{:S(2)}) collective-permute-start(bf16[512,2048]{1,0:T(8,128)(2,1)} %get-tuple-element.66), channel_id=1, source_target_pairs={{0,3},{1,0},{2,1},{3,2},{4,7},{5,4},{6,5},{7,6},{8,11},{9,8},{10,9... | collective-permute-start | bytes 6291464 | tf_op jit(solution)/shard_map/ppermute | solution.py:118
  147.7 53.2 %collective-permute-start.4 = (bf16[512,2048]{1,0:T(8,128)(2,1)}, bf16[512,2048]{1,0:T(8,128)(2,1)}, u32[]{:S(2)}, u32[]{:S(2)}) collective-permute-start(bf16[512,2048]{1,0:T(8,128)(2,1)} %get-tuple-element.66), channel_id=1, source_target_pairs={{0,1},{1,2},{2,3},{3,0},{4,5},{5,6},{6,7},{7,4},{8,9},{9,10},{10,1... | collective-permute-start | bytes 6291464 | tf_op jit(solution)/shard_map/ppermute | solution.py:117
  149.7 43.9 %collective-permute-start.2 = (f32[512]{0:T(512)S(1)}, f32[512]{0:T(512)S(1)}, u32[]{:S(2)}, u32[]{:S(2)}) collective-permute-start(f32[512]{0:T(512)S(1)} %get-tuple-element.65), channel_id=1, source_target_pairs={{0,3},{1,0},{2,1},{3,2},{4,7},{5,4},{6,5},{7,6},{8,11},{9,8},{10,9... | collective-permute-start | bytes 6152 | tf_op jit(solution)/shard_map/ppermute | solution.py:106
  153.0 43.0 %collective-permute-start.1 = (f32[512]{0:T(512)S(1)}, f32[512]{0:T(512)S(1)}, u32[]{:S(2)}, u32[]{:S(2)}) collective-permute-start(f32[512]{0:T(512)S(1)} %get-tuple-element.65), channel_id=1, source_target_pairs={{0,2},{1,3},{2,0},{3,1},{4,6},{5,7},{6,4},{7,5},{8,10},{9,11},{10,... | collective-permute-start | bytes 6152 | tf_op jit(solution)/shard_map/ppermute | solution.py:106
  193.5 5.1 %collective-permute-start = (f32[512]{0:T(512)S(1)}, f32[512]{0:T(512)S(1)}, u32[]{:S(2)}, u32[]{:S(2)}) collective-permute-start(f32[512]{0:T(512)S(1)} %get-tuple-element.65), channel_id=1, source_target_pairs={{0,1},{1,2},{2,3},{3,0},{4,5},{5,6},{6,7},{7,4},{8,9},{9,10},{10,1... | collective-permute-start | bytes 6152 | tf_op jit(solution)/shard_map/ppermute | solution.py:106
  198.8 23.8 %collective-permute-start.7 = (bf16[512,1024]{1,0:T(8,128)(2,1)S(1)}, bf16[512,1024]{1,0:T(8,128)(2,1)S(1)}, u32[]{:S(2)}, u32[]{:S(2)}) collective-permute-start(bf16[512,1024]{1,0:T(8,128)(2,1)S(1)} %slice.235), channel_id=1, source_target_pairs={{0,3},{1,0},{2,1},{3,2},{4,7},{5,4},{6,5},{7,6},{8,11},{9,8},{10,9... | collective-permute-start | bytes 3145736 | tf_op jit(solution)/shard_map/ppermute | solution.py:120
  202.2 24.6 %collective-permute-start.6 = (bf16[512,1024]{1,0:T(8,128)(2,1)S(1)}, bf16[512,1024]{1,0:T(8,128)(2,1)S(1)}, u32[]{:S(2)}, u32[]{:S(2)}) collective-permute-start(bf16[512,1024]{1,0:T(8,128)(2,1)S(1)} %slice.234), channel_id=1, source_target_pairs={{0,1},{1,2},{2,3},{3,0},{4,5},{5,6},{6,7},{7,4},{8,9},{9,10},{10,1... | collective-permute-start | bytes 3145736 | tf_op jit(solution)/shard_map/ppermute | solution.py:119
  227.6 1.0 copy-start.8
  227.6 1.0 copy-start.9
  227.6 1.1 copy-start.10
  227.6 1.2 copy-start.11
  227.6 1.2 copy-start.12
  227.7 1.3 copy-start.13
  227.7 1.4 copy-start.14
  227.7 1.4 copy-start.15
  229.1 3.5 %copy-start.16 = (bf16[512,256]{1,0:T(8,128)(2,1)S(1)}, bf16[512,256]{1,0:T(8,128)(2,1)}, u32[]{:S(2)}) copy-start(bf16[512,256]{1,0:T(8,128)(2,1)} %get-tuple-element.69) | copy-start | bytes 786436
  229.1 3.5 %copy-start.17 = (bf16[512,256]{1,0:T(8,128)(2,1)S(1)}, bf16[512,256]{1,0:T(8,128)(2,1)}, u32[]{:S(2)}) copy-start(bf16[512,256]{1,0:T(8,128)(2,1)} %get-tuple-element.70) | copy-start | bytes 786436
  229.1 3.5 %copy-start.18 = (bf16[512,256]{1,0:T(8,128)(2,1)S(1)}, bf16[512,256]{1,0:T(8,128)(2,1)}, u32[]{:S(2)}) copy-start(bf16[512,256]{1,0:T(8,128)(2,1)} %get-tuple-element.71) | copy-start | bytes 786436
  229.1 3.5 %copy-start.19 = (bf16[512,256]{1,0:T(8,128)(2,1)S(1)}, bf16[512,256]{1,0:T(8,128)(2,1)}, u32[]{:S(2)}) copy-start(bf16[512,256]{1,0:T(8,128)(2,1)} %get-tuple-element.72) | copy-start | bytes 786436
  229.1 3.5 %copy-start.20 = (bf16[512,256]{1,0:T(8,128)(2,1)S(1)}, bf16[512,256]{1,0:T(8,128)(2,1)}, u32[]{:S(2)}) copy-start(bf16[512,256]{1,0:T(8,128)(2,1)} %get-tuple-element.73) | copy-start | bytes 786436
  229.1 3.5 %copy-start.21 = (bf16[512,256]{1,0:T(8,128)(2,1)S(1)}, bf16[512,256]{1,0:T(8,128)(2,1)}, u32[]{:S(2)}) copy-start(bf16[512,256]{1,0:T(8,128)(2,1)} %get-tuple-element.74) | copy-start | bytes 786436
  229.2 3.5 %copy-start.22 = (bf16[512,256]{1,0:T(8,128)(2,1)S(1)}, bf16[512,256]{1,0:T(8,128)(2,1)}, u32[]{:S(2)}) copy-start(bf16[512,256]{1,0:T(8,128)(2,1)} %get-tuple-element.75) | copy-start | bytes 786436
  229.2 3.5 %copy-start.23 = (bf16[512,256]{1,0:T(8,128)(2,1)S(1)}, bf16[512,256]{1,0:T(8,128)(2,1)}, u32[]{:S(2)}) copy-start(bf16[512,256]{1,0:T(8,128)(2,1)} %get-tuple-element.76) | copy-start | bytes 786436
  229.2 7.2 %slice-start = ((s8[10485760]{0:T(1024)(128)(4,1)}), s8[4194304]{0:T(1024)(128)(4,1)S(1)}, s32[]{:S(2)}) async-start(s8[10485760]{0:T(1024)(128)(4,1)} %bitcast.115), calls=%async_computation.2 | async-start | bytes 8388608
  229.2 7.2 %slice-start.1 = ((s8[10485760]{0:T(1024)(128)(4,1)}), s8[4194304]{0:T(1024)(128)(4,1)S(1)}, s32[]{:S(2)}) async-start(s8[10485760]{0:T(1024)(128)(4,1)} %bitcast.115), calls=%async_computation.3 | async-start | bytes 8388608
  232.7 3.6 %copy-start.2 = (bf16[512,256]{1,0:T(8,128)(2,1)S(1)}, bf16[512,256]{1,0:T(8,128)(2,1)}, u32[]{:S(2)}) copy-start(bf16[512,256]{1,0:T(8,128)(2,1)} %get-tuple-element.29) | copy-start | bytes 786436
  232.7 3.6 %copy-start.3 = (bf16[512,256]{1,0:T(8,128)(2,1)S(1)}, bf16[512,256]{1,0:T(8,128)(2,1)}, u32[]{:S(2)}) copy-start(bf16[512,256]{1,0:T(8,128)(2,1)} %get-tuple-element.30) | copy-start | bytes 786436
  232.7 3.6 %copy-start.4 = (bf16[512,256]{1,0:T(8,128)(2,1)S(1)}, bf16[512,256]{1,0:T(8,128)(2,1)}, u32[]{:S(2)}) copy-start(bf16[512,256]{1,0:T(8,128)(2,1)} %get-tuple-element.31) | copy-start | bytes 786436
  232.7 3.6 %copy-start.5 = (bf16[512,256]{1,0:T(8,128)(2,1)S(1)}, bf16[512,256]{1,0:T(8,128)(2,1)}, u32[]{:S(2)}) copy-start(bf16[512,256]{1,0:T(8,128)(2,1)} %get-tuple-element.32) | copy-start | bytes 786436
  232.8 3.6 %copy-start.6 = (bf16[512,256]{1,0:T(8,128)(2,1)S(1)}, bf16[512,256]{1,0:T(8,128)(2,1)}, u32[]{:S(2)}) copy-start(bf16[512,256]{1,0:T(8,128)(2,1)} %get-tuple-element.33) | copy-start | bytes 786436
  232.8 3.6 %copy-start.7 = (bf16[512,256]{1,0:T(8,128)(2,1)S(1)}, bf16[512,256]{1,0:T(8,128)(2,1)}, u32[]{:S(2)}) copy-start(bf16[512,256]{1,0:T(8,128)(2,1)} %get-tuple-element.34) | copy-start | bytes 786436
  232.8 3.6 %slice-start.2 = ((s8[10485760]{0:T(1024)(128)(4,1)}), s8[2097152]{0:T(1024)(128)(4,1)S(1)}, s32[]{:S(2)}) async-start(s8[10485760]{0:T(1024)(128)(4,1)} %bitcast.115), calls=%async_computation.4 | async-start | bytes 4194304
  249.8 3.3 %copy-start.26 = (f32[1024]{0:T(1024)S(1)}, f32[1024]{0:T(1024)}, u32[]{:S(2)}) copy-start(f32[1024]{0:T(1024)} %param.17) | copy-start | bytes 12292
  253.9 0.7 copy-start.27
  258.9 1.8 copy-start.28
  260.6 4.0 %copy-start.1 = (bf16[512,2048]{1,0:T(8,128)(2,1)S(1)}, bf16[512,2048]{1,0:T(8,128)(2,1)}, u32[]{:S(2)}) copy-start(bf16[512,2048]{1,0:T(8,128)(2,1)} %param.10) | copy-start | bytes 6291460
Sparse Core Ops, SparseCore 0:
  9.5 82.9 all-gather.2
where the time goes:
time: 272 us; the launch traced here: 271 us
  waiting for transfers between devices  139 us (51%)
  blocking collectives  44.7 us (16%)
  matrix products  35.5 us (13%)
  other arithmetic  18 us (7%)
  between operations  14.1 us (5%)
  local copies, waits for them, and re-layouts  10.9 us (4%)
  starting transfers between devices  9.45 us (3%)
    all_gather x1, waiting for transfers between devices, body(): own_weights = lax.all_gather(weights, CHIPS, axis=0, tiled=False)  77.7 us
    all_to_all x1, blocking collectives, body(): lax.all_to_all(payload, SEQ, split_axis=0, concat_axis=0, tiled=True)  44.7 us
    ppermute x3, waiting for transfers between devices, body(): lax.ppermute(own_sq, TP, [(t, (t + k) % tp_count) for t in range(tp_count)])  44.6 us
    dot_general x8, matrix products, project(): part = jnp.dot(cols, rows, preferred_element_type=jnp.float32)  23.6 us
    ppermute x1, waiting for transfers between devices, body(): far_b = lax.ppermute(from_right[:, half:], TP, to_left)  12.2 us
  transfers between devices with their start and end apart: 9, of which 6 were waited for; matrix products, arithmetic and copies ran while one was open for 13% of the time, Pallas kernels for 0%

commit v1 on v0

--- a/solution.py
+++ b/solution.py
@@ -79,10 +79,15 @@
             ],
             axis=1,
         )
+        block = width // (4 * core_count)
+        span = 4 * block
+        by_core = (
+            rollout_rows.reshape(row_count, 4, core_count, block).transpose(0, 2, 1, 3).reshape(row_count, width)
+        )
         picked = jnp.einsum(
             "psr,rf->psf",
             slot_hits.astype(jnp.bfloat16),
-            rollout_rows,
+            by_core,
             preferred_element_type=jnp.float32,
         ).astype(jnp.bfloat16)
         payload = jnp.concatenate([picked, tag_row[:, None, :]], axis=1)
@@ -121,20 +126,16 @@
         far = jnp.concatenate([far_a, far_b], axis=1)
         pieces = [learner_part, from_left, far, from_right]
 
-        block = width // (4 * core_count)
-        span = 4 * block
         own_rows = own_weights.reshape(tp_count, span, own_weights.shape[-1])
         other_rows = other_weights.reshape(tp_count, span, own_weights.shape[-1])
 
         def core_block(x, c):
-            return jnp.concatenate(
-                [x[:, (hl * core_count + c) * block : (hl * core_count + c + 1) * block] for hl in range(4)],
-                axis=1,
-            )
+            return x[:, c * span : (c + 1) * span]
 
         def normalize(piece, k, scale, norm_gain, tp_index):
             quarter = (tp_index - k) % tp_count
             gain = lax.dynamic_slice_in_dim(norm_gain, quarter * width, width)
+            gain = gain.reshape(4, core_count, block).transpose(1, 0, 2).reshape(width)
             return (piece.astype(jnp.float32) * scale * gain).astype(jnp.bfloat16)
 
         def project(normed, k, tp_index, core_index):

time: 272 us -> 282 us (1.037)
  the two profiles are of different devices: /device:TPU:0 before, /device:TPU:49 now
where the time goes in v1:
time: 282 us; the launch traced here: 278 us
  waiting for transfers between devices  139 us (49%)
  blocking collectives  43.6 us (15%)
  matrix products  36 us (13%)
  other arithmetic  20.6 us (7%)
  local copies, waits for them, and re-layouts  16.5 us (6%)
  between operations  14 us (5%)
  starting transfers between devices  8.48 us (3%)
    all_gather x1, waiting for transfers between devices, body(): own_weights = lax.all_gather(weights, CHIPS, axis=0, tiled=False)  79.4 us
    all_to_all x1, blocking collectives, body(): lax.all_to_all(payload, SEQ, split_axis=0, concat_axis=0, tiled=True)  43.6 us
    ppermute x1, waiting for transfers between devices, body(): from_right = lax.ppermute(learner_part, TP, to_left)  39.9 us
    dot_general x8, matrix products, project(): part = jnp.dot(cols, rows, preferred_element_type=jnp.float32)  24 us
    ppermute x1, waiting for transfers between devices, body(): far_b = lax.ppermute(from_right[:, half:], TP, to_left)  13.3 us
    convert_element_type x2, other arithmetic, normalize(): return (piece.astype(jnp.float32) * scale * gain).astype(jnp.bfloat16)  7.28 us
  transfers between devices with their start and end apart: 9, of which 5 were waited for; matrix products, arithmetic and copies ran while one was open for 15% of the time, Pallas kernels for 0%

profile of v1, /device:TPU:49, one launch (start us, length us, event | category | flops | bytes accessed | tf_op | source)
XLA Modules:
  0.0 277.9 jit_solution(18256600447699323807)
XLA Ops:
  6.5 2.1 pad_maximum_fusion.2
  8.7 0.0 all-gather.3.cloned.1.call-update
  8.7 0.7 add_select_fusion.3
  9.4 1.2 reduce-window.15
  10.6 0.2 slice_reduce_fusion
  10.8 79.4 %all-gather.3.cloned.1.call-done = bf16[4096,1280]{1,0:T(8,128)(2,1)} async-done(((bf16[256,1280]{1,0:T(8,128)(2,1)}), bf16[4096,1280]{1,0:T(8,128)(2,1)}) %all-gather.3.cloned.1.call-update) | async-done | bytes 10485776 | tf_op jit(solution)/shard_map/all_gather | solution.py:59
  90.3 0.8 collective-permute-start.3
  91.1 0.1 fusion.104
  91.2 0.4 fusion.45
  91.7 0.1 copy.40
  91.8 2.8 reshape.323
  94.5 2.7 copy.39
  97.2 2.8 reshape.339
  100.0 0.1 concatenate.34
  100.2 3.1 %convolution_convert_fusion = bf16[32,20,2048]{2,0,1:T(8,128)(2,1)S(1)} fusion(bf16[512,2048,1]{1,0,2:T(8,128)(2,1)} %reshape.339, pred[20,512]{1,0:T(8,128)(4,1)S(1)} %iota_compare_fusion.6, pred[32,512]{1,0:T(8,128)(4,1)S(1)} %iota_compare_fusion.5), kind=kOutput, calls=%fused_computation.22 | convolution fusion | flops 1343815680 | bytes 4745216 | tf_op jit(solution)/shard_map/psr,rf->psf/dot_general | solution.py:87
  103.3 0.2 pad_maximum_fusion
  103.6 1.5 copy.44
  105.1 43.6 %all_to_all.5 = bf16[32,21,2048]{2,1,0:T(8,128)(2,1)S(1)} all-to-all(bf16[32,21,2048]{2,1,0:T(8,128)(2,1)S(1)} %copy.44), channel_id=1, replica_groups=mesh['chips'=16,'core'=2,'tp'=4] {'chips','core'}, dimensions={0} | all-to-all | bytes 5505024 | tf_op jit(solution)/shard_map/all_to_all | solution.py:94
  148.7 0.1 fusion.108
  148.8 0.1 copy.46
  148.8 4.0 %fusion.2 = (f32[512]{0:T(512)S(1)}, bf16[512,2048]{1,0:T(8,128)(2,1)}) fusion(bf16[32,20,2048]{2,1,0:T(8,128)(2,1)S(1)} %bitcast.132, s32[32,20]{0,1:T(8,128)S(1)} %copy.46), kind=kOutput, calls=%fused_computation.7 | convolution fusion | flops 1346698752 | bytes 4723200 | tf_op jit(solution)/shard_map/rps,psf->rf/dot_general | solution.py:99
  152.8 2.4 collective-permute-start.5
  155.3 0.1 slice_compare_fusion
  155.3 0.1 add_select_fusion.4
  155.4 0.3 reduce-window.19
  155.7 0.1 slice.103
  155.8 0.1 slice_reduce_fusion.1
  156.0 0.1 fusion.113
  156.0 0.2 fusion.58
  156.3 1.8 multiply_cosine_fusion
  158.1 2.7 collective-permute-start.2
  160.8 39.9 %collective-permute-done.5 = bf16[512,2048]{1,0:T(8,128)(2,1)S(1)} collective-permute-done((bf16[512,2048]{1,0:T(8,128)(2,1)}, bf16[512,2048]{1,0:T(8,128)(2,1)S(1)}, u32[]{:S(2)}, u32[]{:S(2)}) %collective-permute-start.5) | collective-permute-done | bytes 2097184 | tf_op jit(solution)/shard_map/ppermute | solution.py:123
  200.7 1.1 collective-permute-start
  201.8 0.1 slice.121
  201.9 2.1 collective-permute-done.4
  204.0 0.4 collective-permute-start.7
  204.3 2.3 slice.120
  206.6 1.1 collective-permute-start.6
  207.9 6.7 %fusion.4 = (bf16[512,2048]{1,0:T(8,128)(2,1)}, bf16[512,2048]{1,0:T(8,128)(2,1)}, bf16[512,2048]{1,0:T(8,128)(2,1)}) fusion(bf16[512,2048]{1,0:T(8,128)(2,1)} %get-tuple-element.34, f32[2048]{0:T(1024)S(1)} %bitcast.135, f32[512]{0:T(512)S(1)} %add_rsqrt_fusion, f32[2048]{0:T(1024)S(1)} %bitcast.136, bf16[512,2048]{1,0:T(8,128)(2,1)} %collective-permute-done.4, ...), kind=kLoop, calls=%fused_computation.9 | loop fusion | flops 12582912 | bytes 12609536 | tf_op jit(solution)/shard_map/convert_element_type | solution.py:139
  214.6 13.3 %collective-permute-done.7 = bf16[512,1024]{1,0:T(8,128)(2,1)} collective-permute-done((bf16[512,1024]{1,0:T(8,128)(2,1)S(1)}, bf16[512,1024]{1,0:T(8,128)(2,1)}, u32[]{:S(2)}, u32[]{:S(2)}) %collective-permute-start.7) | collective-permute-done | bytes 1048608 | tf_op jit(solution)/shard_map/ppermute | solution.py:125
  227.9 4.0 %collective-permute-done.6 = bf16[512,1024]{1,0:T(8,128)(2,1)} collective-permute-done((bf16[512,1024]{1,0:T(8,128)(2,1)}, bf16[512,1024]{1,0:T(8,128)(2,1)}, u32[]{:S(2)}, u32[]{:S(2)}) %collective-permute-start.6) | collective-permute-done | bytes 1048608 | tf_op jit(solution)/shard_map/ppermute | solution.py:124
  231.9 1.7 pad_maximum_fusion.1
  233.7 0.5 multiply_convert_fusion
  234.3 1.0 copy-done
  235.3 3.5 %fusion.30 = f32[512,1280]{1,0:T(8,128)S(1)} fusion(bf16[4,1024,1280]{2,1,0:T(8,128)(2,1)} %bitcast.149, s32[]{:T(128)S(6)} %select_n.137, pred[]{:T(512)S(6)} %eq.114, bf16[512,2048]{1,0:T(8,128)(2,1)S(1)} %copy-done), kind=kOutput, calls=%fused_computation.39 | convolution fusion | flops 1342701568 | bytes 7340037 | tf_op jit(solution)/shard_map/dot_general | solution.py:150
  238.8 3.5 %fusion.13 = f32[512,1280]{1,0:T(8,128)S(1)} fusion(bf16[4,1024,1280]{2,1,0:T(8,128)(2,1)} %bitcast.150, s32[]{:T(128)S(6)} %select_n.153, pred[]{:T(512)S(6)} %eq.131, bf16[512,2048]{1,0:T(8,128)(2,1)S(1)} %multiply_convert_fusion), kind=kOutput, calls=%fused_computation.26 | convolution fusion | flops 1342701568 | bytes 7340037 | tf_op jit(solution)/shard_map/dot_general | solution.py:150
  242.3 3.5 %fusion.15 = f32[512,1280]{1,0:T(8,128)S(1)} fusion(bf16[4,1024,1280]{2,1,0:T(8,128)(2,1)} %bitcast.11, s32[]{:T(128)S(6)} %select_n.147, pred[]{:T(512)S(6)} %eq.114, bf16[512,2048]{1,0:T(8,128)(2,1)S(1)} %copy-done.3), kind=kOutput, calls=%fused_computation.28 | convolution fusion | flops 1342701568 | bytes 7340037 | tf_op jit(solution)/shard_map/dot_general | solution.py:150
  245.8 1.6 fusion.19
  247.4 3.3 %fusion.22 = f32[512,1280]{1,0:T(8,128)S(1)} fusion(bf16[4,1024,1280]{2,1,0:T(8,128)(2,1)} %bitcast.11, s32[]{:T(128)S(6)} %select_n.142, pred[]{:T(512)S(6)} %eq.114, bf16[512,2048]{1,0:T(8,128)(2,1)S(1)} %copy-done.2), kind=kOutput, calls=%fused_computation.33 | convolution fusion | flops 1342701568 | bytes 7340037 | tf_op jit(solution)/shard_map/dot_general | solution.py:150
  250.8 1.6 fusion.26
  252.4 3.5 %fusion.10 = f32[512,1280]{1,0:T(8,128)S(1)} fusion(f32[512,1280]{1,0:T(8,128)S(1)} %fusion.19, f32[512,1280]{1,0:T(8,128)S(1)} %fusion.26, f32[512,1280]{1,0:T(8,128)S(1)} %fusion.30, bf16[4,1024,1280]{2,1,0:T(8,128)(2,1)} %bitcast.11, s32[]{:T(128)S(6)} %select_n.137, pred[]{:T(512)S(6)} %eq.114, bf16[512,2048]{1,0:T(8,128)(2,1)S(1)} %copy-done), kind=kOutput, calls=%fused_computation.21 | convolution fusion | flops 1344667648 | bytes 15204357 | tf_op jit(solution)/shard_map/dot_general | solution.py:150
  255.9 0.0 copy-start.8
  255.9 3.6 %fusion.9 = f32[512,1280]{1,0:T(8,128)S(1)} fusion(f32[512,1280]{1,0:T(8,128)S(1)} %fusion.10, f32[512,1280]{1,0:T(8,128)S(1)} %fusion.13, bf16[4,1024,1280]{2,1,0:T(8,128)(2,1)} %bitcast.11, s32[]{:T(128)S(6)} %select_n.153, pred[]{:T(512)S(6)} %eq.131, bf16[512,2048]{1,0:T(8,128)(2,1)S(1)} %multiply_convert_fusion), kind=kOutput, calls=%fused_computation.20 | convolution fusion | flops 1344012288 | bytes 12582917 | tf_op jit(solution)/shard_map/dot_general | solution.py:150
  259.5 0.2 fusion.40
  259.8 0.5 copy.69
  260.3 0.0 copy-start.9
  260.3 0.7 fusion.126
  261.0 1.2 fusion.102
  262.3 0.8 subtract_convert_fusion
  263.1 2.2 fusion.1
  265.3 0.0 copy-start.10
  265.3 1.7 fusion
  267.0 2.7 fusion.42
  269.7 1.3 copy.56
  (59 shorter events, 0.4 us)
Async XLA Ops:
  6.5 85.2 %copy-start.1 = (bf16[512,2048]{1,0:T(8,128)(2,1)S(1)}, bf16[512,2048]{1,0:T(8,128)(2,1)}, u32[]{:S(2)}) copy-start(bf16[512,2048]{1,0:T(8,128)(2,1)} %param.10) | copy-start | bytes 6291460
  6.5 83.7 %all-gather.3.cloned.1.call-start = ((), (), s32[]{:S(2)}) async-start(), calls=%async_computation.1 | async-start | bytes 11141120 | tf_op jit(solution)/shard_map/all_gather | solution.py:59
  90.3 152.0 %collective-permute-start.3 = (bf16[16,256,1280]{2,1,0:T(8,128)(2,1)}, bf16[16,256,1280]{2,1,0:T(8,128)(2,1)}, u32[]{:S(2)}, u32[]{:S(2)}) collective-permute-start(bf16[16,256,1280]{2,1,0:T(8,128)(2,1)} %bitcast.148), channel_id=1, source_target_pairs={{0,4},{4,0},{1,5},{5,1},{2,6},{6,2},{3,7},{7,3},{8,12},{12,8},{9,1... | collective-permute-start | bytes 31457288 | tf_op jit(solution)/shard_map/ppermute | solution.py:60
  148.8 6.4 %copy-start.6 = (s32[512]{0:T(512)S(1)}, s32[512]{0:T(512)}, u32[]{:S(2)}) copy-start(s32[512]{0:T(512)} %param.12) | copy-start | bytes 6148
  152.8 54.9 %copy-start.7 = (f32[8192]{0:T(1024)S(1)}, f32[8192]{0:T(1024)}, u32[]{:S(2)}) copy-start(f32[8192]{0:T(1024)} %param.13) | copy-start | bytes 98308
  152.8 47.9 %collective-permute-start.5 = (bf16[512,2048]{1,0:T(8,128)(2,1)}, bf16[512,2048]{1,0:T(8,128)(2,1)S(1)}, u32[]{:S(2)}, u32[]{:S(2)}) collective-permute-start(bf16[512,2048]{1,0:T(8,128)(2,1)} %get-tuple-element.34), channel_id=1, source_target_pairs={{0,3},{1,0},{2,1},{3,2},{4,7},{5,4},{6,5},{7,6},{8,11},{9,8},{10,9... | collective-permute-start | bytes 6291464 | tf_op jit(solution)/shard_map/ppermute | solution.py:123
  155.3 48.7 %collective-permute-start.4 = (bf16[512,2048]{1,0:T(8,128)(2,1)}, bf16[512,2048]{1,0:T(8,128)(2,1)}, u32[]{:S(2)}, u32[]{:S(2)}) collective-permute-start(bf16[512,2048]{1,0:T(8,128)(2,1)} %get-tuple-element.34), channel_id=1, source_target_pairs={{0,1},{1,2},{2,3},{3,0},{4,5},{5,6},{6,7},{7,4},{8,9},{9,10},{10,1... | collective-permute-start | bytes 6291464 | tf_op jit(solution)/shard_map/ppermute | solution.py:122
  158.1 48.5 %collective-permute-start.2 = (f32[512]{0:T(512)S(1)}, f32[512]{0:T(512)S(1)}, u32[]{:S(2)}, u32[]{:S(2)}) collective-permute-start(f32[512]{0:T(512)S(1)} %get-tuple-element.33), channel_id=1, source_target_pairs={{0,3},{1,0},{2,1},{3,2},{4,7},{5,4},{6,5},{7,6},{8,11},{9,8},{10,9... | collective-permute-start | bytes 6152 | tf_op jit(solution)/shard_map/ppermute | solution.py:111
  160.8 47.1 %collective-permute-start.1 = (f32[512]{0:T(512)S(1)}, f32[512]{0:T(512)S(1)}, u32[]{:S(2)}, u32[]{:S(2)}) collective-permute-start(f32[512]{0:T(512)S(1)} %get-tuple-element.33), channel_id=1, source_target_pairs={{0,2},{1,3},{2,0},{3,1},{4,6},{5,7},{6,4},{7,5},{8,10},{9,11},{10,... | collective-permute-start | bytes 6152 | tf_op jit(solution)/shard_map/ppermute | solution.py:111
  200.7 7.2 %collective-permute-start = (f32[512]{0:T(512)S(1)}, f32[512]{0:T(512)S(1)}, u32[]{:S(2)}, u32[]{:S(2)}) collective-permute-start(f32[512]{0:T(512)S(1)} %get-tuple-element.33), channel_id=1, source_target_pairs={{0,1},{1,2},{2,3},{3,0},{4,5},{5,6},{6,7},{7,4},{8,9},{9,10},{10,1... | collective-permute-start | bytes 6152 | tf_op jit(solution)/shard_map/ppermute | solution.py:111
  204.0 23.9 %collective-permute-start.7 = (bf16[512,1024]{1,0:T(8,128)(2,1)S(1)}, bf16[512,1024]{1,0:T(8,128)(2,1)}, u32[]{:S(2)}, u32[]{:S(2)}) collective-permute-start(bf16[512,1024]{1,0:T(8,128)(2,1)S(1)} %slice.121), channel_id=1, source_target_pairs={{0,3},{1,0},{2,1},{3,2},{4,7},{5,4},{6,5},{7,6},{8,11},{9,8},{10,9... | collective-permute-start | bytes 3145736 | tf_op jit(solution)/shard_map/ppermute | solution.py:125
  206.6 25.3 %collective-permute-start.6 = (bf16[512,1024]{1,0:T(8,128)(2,1)}, bf16[512,1024]{1,0:T(8,128)(2,1)}, u32[]{:S(2)}, u32[]{:S(2)}) collective-permute-start(bf16[512,1024]{1,0:T(8,128)(2,1)} %slice.120), channel_id=1, source_target_pairs={{0,1},{1,2},{2,3},{3,0},{4,5},{5,6},{6,7},{7,4},{8,9},{9,10},{10,1... | collective-permute-start | bytes 3145736 | tf_op jit(solution)/shard_map/ppermute | solution.py:124
  233.7 1.6 copy-start
  235.3 10.5 %slice-start = ((s8[10485760]{0:T(1024)(128)(4,1)}), s8[4194304]{0:T(1024)(128)(4,1)S(1)}, s32[]{:S(2)}) async-start(s8[10485760]{0:T(1024)(128)(4,1)} %bitcast.151), calls=%async_computation.2 | async-start | bytes 8388608
  238.8 3.5 %copy-start.3 = (bf16[512,2048]{1,0:T(8,128)(2,1)S(1)}, bf16[512,2048]{1,0:T(8,128)(2,1)}, u32[]{:S(2)}) copy-start(bf16[512,2048]{1,0:T(8,128)(2,1)} %get-tuple-element.30) | copy-start | bytes 6291460
  238.8 7.0 %slice-start.1 = ((s8[10485760]{0:T(1024)(128)(4,1)}), s8[4194304]{0:T(1024)(128)(4,1)S(1)}, s32[]{:S(2)}) async-start(s8[10485760]{0:T(1024)(128)(4,1)} %bitcast.151), calls=%async_computation.3 | async-start | bytes 8388608
  242.3 3.5 %slice-start.2 = ((s8[10485760]{0:T(1024)(128)(4,1)}), s8[2097152]{0:T(1024)(128)(4,1)S(1)}, s32[]{:S(2)}) async-start(s8[10485760]{0:T(1024)(128)(4,1)} %bitcast.151), calls=%async_computation.4 | async-start | bytes 4194304
  245.8 1.6 copy-start.2
  255.9 3.7 %copy-start.8 = (f32[1024]{0:T(1024)S(1)}, f32[1024]{0:T(1024)}, u32[]{:S(2)}) copy-start(f32[1024]{0:T(1024)} %param.17) | copy-start | bytes 12292
  260.3 0.7 copy-start.9
  260.3 2.0 copy-start.4
  260.3 2.0 copy-start.5
  265.3 1.8 copy-start.10
Sparse Core Ops, SparseCore 0:
  9.5 80.7 all-gather.2

commit v2 on v0

--- a/solution.py
+++ b/solution.py
@@ -113,12 +113,12 @@
 
         to_right = [(t, (t + 1) % tp_count) for t in range(tp_count)]
         to_left = [(t, (t - 1) % tp_count) for t in range(tp_count)]
-        half = width // 2
+        half_rows = row_count // 2
         from_left = lax.ppermute(learner_part, TP, to_right)
         from_right = lax.ppermute(learner_part, TP, to_left)
-        far_a = lax.ppermute(from_left[:, :half], TP, to_right)
-        far_b = lax.ppermute(from_right[:, half:], TP, to_left)
-        far = jnp.concatenate([far_a, far_b], axis=1)
+        far_a = lax.ppermute(from_left[:half_rows], TP, to_right)
+        far_b = lax.ppermute(from_right[half_rows:], TP, to_left)
+        far = jnp.concatenate([far_a, far_b], axis=0)
         pieces = [learner_part, from_left, far, from_right]
 
         block = width // (4 * core_count)

time: 272 us -> 272 us (level)
  the two profiles are of different devices: /device:TPU:0 before, /device:TPU:49 now
where the time goes in v2:
time: 272 us; the launch traced here: 266 us
  waiting for transfers between devices  135 us (50%)
  blocking collectives  43.6 us (16%)
  matrix products  35.5 us (13%)
  other arithmetic  17.9 us (7%)
  between operations  14.1 us (5%)
  local copies, waits for them, and re-layouts  10.9 us (4%)
  starting transfers between devices  8.91 us (3%)
    all_gather x1, waiting for transfers between devices, body(): own_weights = lax.all_gather(weights, CHIPS, axis=0, tiled=False)  75.5 us
    ppermute x3, waiting for transfers between devices, body(): lax.ppermute(own_sq, TP, [(t, (t + k) % tp_count) for t in range(tp_count)])  44.1 us
    all_to_all x1, blocking collectives, body(): lax.all_to_all(payload, SEQ, split_axis=0, concat_axis=0, tiled=True)  43.6 us
    dot_general x8, matrix products, project(): part = jnp.dot(cols, rows, preferred_element_type=jnp.float32)  23.6 us
    ppermute x1, waiting for transfers between devices, body(): far_b = lax.ppermute(from_right[half_rows:], TP, to_left)  12.2 us
  transfers between devices with their start and end apart: 9, of which 6 were waited for; matrix products, arithmetic and copies ran while one was open for 13% of the time, Pallas kernels for 0%

profile of v2, /device:TPU:49, one launch (start us, length us, event | category | flops | bytes accessed | tf_op | source)
XLA Modules:
  0.0 266.5 jit_solution(17023349867088052235)
XLA Ops:
  6.5 2.1 pad_maximum_fusion.10
  8.7 0.7 add_select_fusion.3
  9.4 1.2 reduce-window.15
  10.6 0.2 slice_reduce_fusion
  10.8 0.1 fusion.81
  11.0 0.4 fusion.38
  11.4 0.1 copy.25
  11.6 0.1 concatenate.58
  11.7 3.0 %convolution_convert_fusion = bf16[32,20,2048]{2,0,1:T(8,128)(2,1)} fusion(bf16[512,2048]{1,0:T(8,128)(2,1)S(1)} %copy-done, pred[20,512]{1,0:T(8,128)(4,1)S(1)} %iota_compare_fusion.6, pred[32,512]{1,0:T(8,128)(4,1)S(1)} %iota_compare_fusion.5), kind=kOutput, calls=%fused_computation.24 | convolution fusion | flops 1343815680 | bytes 4745216 | tf_op jit(solution)/shard_map/psr,rf->psf/dot_general | solution.py:82
  14.8 75.5 %all-gather.3.cloned.1.call-done = bf16[4096,1280]{1,0:T(8,128)(2,1)} async-done(((bf16[256,1280]{1,0:T(8,128)(2,1)}), bf16[4096,1280]{1,0:T(8,128)(2,1)}) %all-gather.3.cloned.1.call-update) | async-done | bytes 10485776 | tf_op jit(solution)/shard_map/all_gather | solution.py:59
  90.3 0.8 collective-permute-start.3
  91.1 2.0 pad_maximum_fusion
  93.1 1.5 copy.29
  94.6 43.6 %all_to_all.5 = bf16[32,21,2048]{2,1,0:T(8,128)(2,1)S(1)} all-to-all(bf16[32,21,2048]{2,1,0:T(8,128)(2,1)S(1)} %copy.29), channel_id=1, replica_groups=mesh['chips'=16,'core'=2,'tp'=4] {'chips','core'}, dimensions={0} | all-to-all | bytes 5505024 | tf_op jit(solution)/shard_map/all_to_all | solution.py:89
  138.3 0.1 copy.31
  138.4 4.0 %fusion.2 = (f32[512]{0:T(512)S(1)}, bf16[512,2048]{1,0:T(8,128)(2,1)}) fusion(bf16[32,20,2048]{2,1,0:T(8,128)(2,1)S(1)} %bitcast.108, s32[32,20]{0,1:T(8,128)S(1)} %copy.31), kind=kOutput, calls=%fused_computation.7 | convolution fusion | flops 1346698752 | bytes 4723200 | tf_op jit(solution)/shard_map/rps,psf->rf/dot_general | solution.py:94
  142.4 2.4 collective-permute-start.5
  144.9 0.1 add_select_fusion.4
  145.0 0.3 reduce-window.19
  145.4 0.1 slice_reduce_fusion.1
  145.5 0.1 fusion.90
  145.6 0.2 fusion.51
  145.8 1.0 multiply_cosine_fusion
  146.8 2.7 %collective-permute-start.2 = (f32[512]{0:T(512)S(1)}, f32[512]{0:T(512)S(1)}, u32[]{:S(2)}, u32[]{:S(2)}) collective-permute-start(f32[512]{0:T(512)S(1)} %get-tuple-element.65), channel_id=1, source_target_pairs={{0,3},{1,0},{2,1},{3,2},{4,7},{5,4},{6,5},{7,6},{8,11},{9,8},{10,9... | collective-permute-start | bytes 6152 | tf_op jit(solution)/shard_map/ppermute | solution.py:106
  149.6 40.7 %collective-permute-done.2 = f32[512]{0:T(512)S(1)} collective-permute-done((f32[512]{0:T(512)S(1)}, f32[512]{0:T(512)S(1)}, u32[]{:S(2)}, u32[]{:S(2)}) %collective-permute-start.2) | collective-permute-done | bytes 2080 | tf_op jit(solution)/shard_map/ppermute | solution.py:106
  190.3 1.1 collective-permute-start
  191.4 0.8 collective-permute-done.1
  192.2 2.5 collective-permute-done
  194.8 1.5 collective-permute-start.7
  196.4 1.3 slice.234
  197.7 0.3 collective-permute-start.6
  198.0 4.7 %fusion.4 = (bf16[512,2048]{1,0:T(8,128)(2,1)S(1)}, bf16[512,2048]{1,0:T(8,128)(2,1)S(1)}, bf16[512,2048]{1,0:T(8,128)(2,1)S(1)}) fusion(bf16[512,2048]{1,0:T(8,128)(2,1)} %get-tuple-element.66, f32[2048]{0:T(1024)S(1)} %get-tuple-element.53, f32[512]{0:T(512)S(1)} %add_rsqrt_fusion, f32[2048]{0:T(1024)S(1)} %get-tuple-element.54, ...), kind=kLoop, calls=%fused_computation.9 | loop fusion | flops 12582912 | bytes 12609536 | tf_op jit(solution)/shard_map/convert_element_type | solution.py:138
  202.7 1.3 fusion.115
  204.0 1.9 fusion.113
  205.9 12.2 %collective-permute-done.7 = bf16[256,2048]{1,0:T(8,128)(2,1)S(1)} collective-permute-done((bf16[256,2048]{1,0:T(8,128)(2,1)S(1)}, bf16[256,2048]{1,0:T(8,128)(2,1)S(1)}, u32[]{:S(2)}, u32[]{:S(2)}) %collective-permute-start.7) | collective-permute-done | bytes 1048608 | tf_op jit(solution)/shard_map/ppermute | solution.py:120
  218.1 3.7 %collective-permute-done.6 = bf16[256,2048]{1,0:T(8,128)(2,1)S(1)} collective-permute-done((bf16[256,2048]{1,0:T(8,128)(2,1)S(1)}, bf16[256,2048]{1,0:T(8,128)(2,1)S(1)}, u32[]{:S(2)}, u32[]{:S(2)}) %collective-permute-start.6) | collective-permute-done | bytes 1048608 | tf_op jit(solution)/shard_map/ppermute | solution.py:119
  221.8 0.1 pad_maximum_fusion.1
  222.0 0.5 multiply_convert_fusion
  222.7 0.1 fusion.112
  222.8 0.7 copy-done.8
  223.5 0.1 copy-done.9
  223.6 0.1 copy-done.10
  223.7 0.1 copy-done.11
  223.8 0.1 copy-done.12
  223.8 0.1 copy-done.13
  223.9 0.1 copy-done.14
  224.0 0.1 copy-done.15
  224.2 3.4 %fusion.16 = f32[512,1280]{1,0:T(8,128)S(1)} fusion(bf16[4,1024,1280]{2,1,0:T(8,128)(2,1)} %bitcast.113, s32[]{:T(128)S(6)} %select_n.147, pred[]{:T(512)S(6)} %eq.114, bf16[512,256]{1,0:T(8,128)(2,1)S(1)} %copy-done.9, bf16[512,256]{1,0:T(8,128)(2,1)S(1)} %copy-done.10, bf16[512,256]{1,0:T(8,128)(2,1)S(1)} %copy-done.11, ...), kind=kOutput, calls=%fused_computation.31 | convolution fusion | flops 1351090176 | bytes 7340037 | tf_op jit(solution)/shard_map/dot_general | solution.py:149
  227.7 3.5 %fusion.19 = f32[512,1280]{1,0:T(8,128)S(1)} fusion(bf16[4,1024,1280]{2,1,0:T(8,128)(2,1)} %bitcast.114, s32[]{:T(128)S(6)} %select_n.142, pred[]{:T(512)S(6)} %eq.114, bf16[512,256]{1,0:T(8,128)(2,1)S(1)} %copy-done.22, bf16[512,256]{1,0:T(8,128)(2,1)S(1)} %copy-done.21, bf16[512,256]{1,0:T(8,128)(2,1)S(1)} %copy-done.20, ...), kind=kOutput, calls=%fused_computation.34 | convolution fusion | flops 1351090176 | bytes 7340037 | tf_op jit(solution)/shard_map/dot_general | solution.py:149
  231.4 1.6 fusion.22
  233.0 1.6 fusion.13
  234.5 3.3 %convolution_add_fusion.1 = f32[512,1280]{1,0:T(8,128)S(1)} fusion(f32[512,1280]{1,0:T(8,128)S(1)} %fusion.16, bf16[4,1024,1280]{2,1,0:T(8,128)(2,1)} %bitcast.10, s32[]{:T(128)S(6)} %select_n.147, pred[]{:T(512)S(6)} %eq.114, bf16[512,256]{1,0:T(8,128)(2,1)S(1)} %copy-done.9, bf16[512,256]{1,0:T(8,128)(2,1)S(1)} %copy-done.10, ...), kind=kOutput, calls=%fused_computation.18 | convolution fusion | flops 1351745536 | bytes 9961477 | tf_op jit(solution)/shard_map/dot_general | solution.py:149
  237.8 3.3 %convolution_add_fusion.2 = f32[512,1280]{1,0:T(8,128)S(1)} fusion(f32[512,1280]{1,0:T(8,128)S(1)} %fusion.19, bf16[4,1024,1280]{2,1,0:T(8,128)(2,1)} %bitcast.10, s32[]{:T(128)S(6)} %select_n.142, pred[]{:T(512)S(6)} %eq.114, bf16[512,256]{1,0:T(8,128)(2,1)S(1)} %copy-done.22, bf16[512,256]{1,0:T(8,128)(2,1)S(1)} %copy-done.21, ...), kind=kOutput, calls=%fused_computation.19 | convolution fusion | flops 1351745536 | bytes 9961477 | tf_op jit(solution)/shard_map/dot_general | solution.py:149
  241.1 3.6 %fusion.10 = f32[512,1280]{1,0:T(8,128)S(1)} fusion(f32[512,1280]{1,0:T(8,128)S(1)} %convolution_add_fusion.1, f32[512,1280]{1,0:T(8,128)S(1)} %convolution_add_fusion.2, f32[512,1280]{1,0:T(8,128)S(1)} %fusion.22, bf16[4,1024,1280]{2,1,0:T(8,128)(2,1)} %bitcast.10, s32[]{:T(128)S(6)} %select_n.137, pred[]{:T(512)S(6)} %eq.114, ...), kind=kOutput, calls=%fused_computation.23 | convolution fusion | flops 1353056256 | bytes 15204357 | tf_op jit(solution)/shard_map/dot_general | solution.py:149
  244.7 3.3 %fusion.9 = f32[512,1280]{1,0:T(8,128)S(1)} fusion(f32[512,1280]{1,0:T(8,128)S(1)} %fusion.10, f32[512,1280]{1,0:T(8,128)S(1)} %fusion.13, bf16[4,1024,1280]{2,1,0:T(8,128)(2,1)} %bitcast.10, s32[]{:T(128)S(6)} %select_n.153, pred[]{:T(512)S(6)} %eq.131, bf16[512,256]{1,0:T(8,128)(2,1)S(1)} %get-tuple-element.20, ...), kind=kOutput, calls=%fused_computation.22 | convolution fusion | flops 1352400896 | bytes 12582917 | tf_op jit(solution)/shard_map/dot_general | solution.py:149
  248.1 0.3 fusion.32
  248.4 0.5 copy.46
  248.9 0.7 fusion.111
  249.6 1.2 fusion.79
  250.8 0.8 subtract_convert_fusion
  251.6 2.2 fusion.1
  253.9 1.7 fusion
  255.6 2.7 %fusion.35 = bf16[128,8,512]{2,0,1:T(8,128)(2,1)S(1)} fusion(f32[8,512]{1,0:T(8,128)S(1)} %fusion, f32[8,512]{1,0:T(8,128)S(1)} %get-tuple-element.67, f32[512,512,8]{1,0,2:T(8,128)S(1)} %get-tuple-element.68, pred[512,512]{0,1:T(8,128)(4,1)S(1)} %fusion.51, f32[512,1280]{1,0:T(8,128)S(1)} %fusion.9, f32[128]{0:T(128)S(1)} %copy-done.28), kind=kOutput, calls=%fused_computation.55 | convolution fusion | flops 548012032 | bytes 9994752 | tf_op jit(solution)/shard_map/kgqp,pkd->qkgd/dot_general | solution.py:191
  258.3 1.3 copy.37
  (83 shorter events, 0.7 us)
Async XLA Ops:
  6.5 5.2 %copy-start = (bf16[512,2048]{1,0:T(8,128)(2,1)S(1)}, bf16[512,2048]{1,0:T(8,128)(2,1)}, u32[]{:S(2)}) copy-start(bf16[512,2048]{1,0:T(8,128)(2,1)} %param.10) | copy-start | bytes 6291460
  6.5 83.7 %all-gather.3.cloned.1.call-start = ((), (), s32[]{:S(2)}) async-start(), calls=%async_computation.1 | async-start | bytes 11141120 | tf_op jit(solution)/shard_map/all_gather | solution.py:59
  90.3 144.3 %collective-permute-start.3 = (bf16[16,256,1280]{2,1,0:T(8,128)(2,1)}, bf16[16,256,1280]{2,1,0:T(8,128)(2,1)}, u32[]{:S(2)}, u32[]{:S(2)}) collective-permute-start(bf16[16,256,1280]{2,1,0:T(8,128)(2,1)} %bitcast.112), channel_id=1, source_target_pairs={{0,4},{4,0},{1,5},{5,1},{2,6},{6,2},{3,7},{7,3},{8,12},{12,8},{9,1... | collective-permute-start | bytes 31457288 | tf_op jit(solution)/shard_map/ppermute | solution.py:60
  138.4 6.5 %copy-start.24 = (s32[512]{0:T(512)S(1)}, s32[512]{0:T(512)}, u32[]{:S(2)}) copy-start(s32[512]{0:T(512)} %param.12) | copy-start | bytes 6148
  138.4 53.0 %copy-start.25 = (f32[8192]{0:T(1024)S(1)}, f32[8192]{0:T(1024)}, u32[]{:S(2)}) copy-start(f32[8192]{0:T(1024)} %param.13) | copy-start | bytes 98308
  142.4 52.3 %collective-permute-start.5 = (bf16[512,2048]{1,0:T(8,128)(2,1)}, bf16[512,2048]{1,0:T(8,128)(2,1)S(1)}, u32[]{:S(2)}, u32[]{:S(2)}) collective-permute-start(bf16[512,2048]{1,0:T(8,128)(2,1)} %get-tuple-element.66), channel_id=1, source_target_pairs={{0,3},{1,0},{2,1},{3,2},{4,7},{5,4},{6,5},{7,6},{8,11},{9,8},{10,9... | collective-permute-start | bytes 6291464 | tf_op jit(solution)/shard_map/ppermute | solution.py:118
  144.8 51.5 %collective-permute-start.4 = (bf16[512,2048]{1,0:T(8,128)(2,1)}, bf16[512,2048]{1,0:T(8,128)(2,1)}, u32[]{:S(2)}, u32[]{:S(2)}) collective-permute-start(bf16[512,2048]{1,0:T(8,128)(2,1)} %get-tuple-element.66), channel_id=1, source_target_pairs={{0,1},{1,2},{2,3},{3,0},{4,5},{5,6},{6,7},{7,4},{8,9},{9,10},{10,1... | collective-permute-start | bytes 6291464 | tf_op jit(solution)/shard_map/ppermute | solution.py:117
  146.8 43.5 %collective-permute-start.2 = (f32[512]{0:T(512)S(1)}, f32[512]{0:T(512)S(1)}, u32[]{:S(2)}, u32[]{:S(2)}) collective-permute-start(f32[512]{0:T(512)S(1)} %get-tuple-element.65), channel_id=1, source_target_pairs={{0,3},{1,0},{2,1},{3,2},{4,7},{5,4},{6,5},{7,6},{8,11},{9,8},{10,9... | collective-permute-start | bytes 6152 | tf_op jit(solution)/shard_map/ppermute | solution.py:106
  149.6 42.7 %collective-permute-start.1 = (f32[512]{0:T(512)S(1)}, f32[512]{0:T(512)S(1)}, u32[]{:S(2)}, u32[]{:S(2)}) collective-permute-start(f32[512]{0:T(512)S(1)} %get-tuple-element.65), channel_id=1, source_target_pairs={{0,2},{1,3},{2,0},{3,1},{4,6},{5,7},{6,4},{7,5},{8,10},{9,11},{10,... | collective-permute-start | bytes 6152 | tf_op jit(solution)/shard_map/ppermute | solution.py:106
  190.3 4.5 %collective-permute-start = (f32[512]{0:T(512)S(1)}, f32[512]{0:T(512)S(1)}, u32[]{:S(2)}, u32[]{:S(2)}) collective-permute-start(f32[512]{0:T(512)S(1)} %get-tuple-element.65), channel_id=1, source_target_pairs={{0,1},{1,2},{2,3},{3,0},{4,5},{5,6},{6,7},{7,4},{8,9},{9,10},{10,1... | collective-permute-start | bytes 6152 | tf_op jit(solution)/shard_map/ppermute | solution.py:106
  194.8 23.3 %collective-permute-start.7 = (bf16[256,2048]{1,0:T(8,128)(2,1)S(1)}, bf16[256,2048]{1,0:T(8,128)(2,1)S(1)}, u32[]{:S(2)}, u32[]{:S(2)}) collective-permute-start(bf16[256,2048]{1,0:T(8,128)(2,1)S(1)} %slice.235), channel_id=1, source_target_pairs={{0,3},{1,0},{2,1},{3,2},{4,7},{5,4},{6,5},{7,6},{8,11},{9,8},{10,9... | collective-permute-start | bytes 3145736 | tf_op jit(solution)/shard_map/ppermute | solution.py:120
  197.7 24.1 %collective-permute-start.6 = (bf16[256,2048]{1,0:T(8,128)(2,1)S(1)}, bf16[256,2048]{1,0:T(8,128)(2,1)S(1)}, u32[]{:S(2)}, u32[]{:S(2)}) collective-permute-start(bf16[256,2048]{1,0:T(8,128)(2,1)S(1)} %slice.234), channel_id=1, source_target_pairs={{0,1},{1,2},{2,3},{3,0},{4,5},{5,6},{6,7},{7,4},{8,9},{9,10},{10,1... | collective-permute-start | bytes 3145736 | tf_op jit(solution)/shard_map/ppermute | solution.py:119
  222.6 1.0 copy-start.8
  222.6 1.0 copy-start.9
  222.6 1.1 copy-start.10
  222.6 1.2 copy-start.11
  222.6 1.2 copy-start.12
  222.6 1.3 copy-start.13
  222.6 1.4 copy-start.14
  222.6 1.4 copy-start.15
  224.1 3.5 %copy-start.16 = (bf16[512,256]{1,0:T(8,128)(2,1)S(1)}, bf16[512,256]{1,0:T(8,128)(2,1)}, u32[]{:S(2)}) copy-start(bf16[512,256]{1,0:T(8,128)(2,1)} %get-tuple-element.69) | copy-start | bytes 786436
  224.1 3.5 %copy-start.17 = (bf16[512,256]{1,0:T(8,128)(2,1)S(1)}, bf16[512,256]{1,0:T(8,128)(2,1)}, u32[]{:S(2)}) copy-start(bf16[512,256]{1,0:T(8,128)(2,1)} %get-tuple-element.70) | copy-start | bytes 786436
  224.1 3.5 %copy-start.18 = (bf16[512,256]{1,0:T(8,128)(2,1)S(1)}, bf16[512,256]{1,0:T(8,128)(2,1)}, u32[]{:S(2)}) copy-start(bf16[512,256]{1,0:T(8,128)(2,1)} %get-tuple-element.71) | copy-start | bytes 786436
  224.1 3.5 %copy-start.19 = (bf16[512,256]{1,0:T(8,128)(2,1)S(1)}, bf16[512,256]{1,0:T(8,128)(2,1)}, u32[]{:S(2)}) copy-start(bf16[512,256]{1,0:T(8,128)(2,1)} %get-tuple-element.72) | copy-start | bytes 786436
  224.1 3.5 %copy-start.20 = (bf16[512,256]{1,0:T(8,128)(2,1)S(1)}, bf16[512,256]{1,0:T(8,128)(2,1)}, u32[]{:S(2)}) copy-start(bf16[512,256]{1,0:T(8,128)(2,1)} %get-tuple-element.73) | copy-start | bytes 786436
  224.1 3.5 %copy-start.21 = (bf16[512,256]{1,0:T(8,128)(2,1)S(1)}, bf16[512,256]{1,0:T(8,128)(2,1)}, u32[]{:S(2)}) copy-start(bf16[512,256]{1,0:T(8,128)(2,1)} %get-tuple-element.74) | copy-start | bytes 786436
  224.1 3.5 %copy-start.22 = (bf16[512,256]{1,0:T(8,128)(2,1)S(1)}, bf16[512,256]{1,0:T(8,128)(2,1)}, u32[]{:S(2)}) copy-start(bf16[512,256]{1,0:T(8,128)(2,1)} %get-tuple-element.75) | copy-start | bytes 786436
  224.1 3.5 %copy-start.23 = (bf16[512,256]{1,0:T(8,128)(2,1)S(1)}, bf16[512,256]{1,0:T(8,128)(2,1)}, u32[]{:S(2)}) copy-start(bf16[512,256]{1,0:T(8,128)(2,1)} %get-tuple-element.76) | copy-start | bytes 786436
  224.1 7.2 %slice-start = ((s8[10485760]{0:T(1024)(128)(4,1)}), s8[4194304]{0:T(1024)(128)(4,1)S(1)}, s32[]{:S(2)}) async-start(s8[10485760]{0:T(1024)(128)(4,1)} %bitcast.115), calls=%async_computation.2 | async-start | bytes 8388608
  224.2 7.1 %slice-start.1 = ((s8[10485760]{0:T(1024)(128)(4,1)}), s8[4194304]{0:T(1024)(128)(4,1)S(1)}, s32[]{:S(2)}) async-start(s8[10485760]{0:T(1024)(128)(4,1)} %bitcast.115), calls=%async_computation.3 | async-start | bytes 8388608
  227.7 3.6 %copy-start.2 = (bf16[512,256]{1,0:T(8,128)(2,1)S(1)}, bf16[512,256]{1,0:T(8,128)(2,1)}, u32[]{:S(2)}) copy-start(bf16[512,256]{1,0:T(8,128)(2,1)} %get-tuple-element.29) | copy-start | bytes 786436
  227.7 3.6 %copy-start.3 = (bf16[512,256]{1,0:T(8,128)(2,1)S(1)}, bf16[512,256]{1,0:T(8,128)(2,1)}, u32[]{:S(2)}) copy-start(bf16[512,256]{1,0:T(8,128)(2,1)} %get-tuple-element.30) | copy-start | bytes 786436
  227.7 3.6 %copy-start.4 = (bf16[512,256]{1,0:T(8,128)(2,1)S(1)}, bf16[512,256]{1,0:T(8,128)(2,1)}, u32[]{:S(2)}) copy-start(bf16[512,256]{1,0:T(8,128)(2,1)} %get-tuple-element.31) | copy-start | bytes 786436
  227.7 3.6 %copy-start.5 = (bf16[512,256]{1,0:T(8,128)(2,1)S(1)}, bf16[512,256]{1,0:T(8,128)(2,1)}, u32[]{:S(2)}) copy-start(bf16[512,256]{1,0:T(8,128)(2,1)} %get-tuple-element.32) | copy-start | bytes 786436
  227.7 3.6 %copy-start.6 = (bf16[512,256]{1,0:T(8,128)(2,1)S(1)}, bf16[512,256]{1,0:T(8,128)(2,1)}, u32[]{:S(2)}) copy-start(bf16[512,256]{1,0:T(8,128)(2,1)} %get-tuple-element.33) | copy-start | bytes 786436
  227.7 3.6 %copy-start.7 = (bf16[512,256]{1,0:T(8,128)(2,1)S(1)}, bf16[512,256]{1,0:T(8,128)(2,1)}, u32[]{:S(2)}) copy-start(bf16[512,256]{1,0:T(8,128)(2,1)} %get-tuple-element.34) | copy-start | bytes 786436
  227.7 3.6 %slice-start.2 = ((s8[10485760]{0:T(1024)(128)(4,1)}), s8[2097152]{0:T(1024)(128)(4,1)S(1)}, s32[]{:S(2)}) async-start(s8[10485760]{0:T(1024)(128)(4,1)} %bitcast.115), calls=%async_computation.4 | async-start | bytes 4194304
  244.7 3.3 %copy-start.26 = (f32[1024]{0:T(1024)S(1)}, f32[1024]{0:T(1024)}, u32[]{:S(2)}) copy-start(f32[1024]{0:T(1024)} %param.17) | copy-start | bytes 12292
  248.9 0.7 copy-start.27
  253.8 1.8 copy-start.28
  255.6 4.0 %copy-start.1 = (bf16[512,2048]{1,0:T(8,128)(2,1)S(1)}, bf16[512,2048]{1,0:T(8,128)(2,1)}, u32[]{:S(2)}) copy-start(bf16[512,2048]{1,0:T(8,128)(2,1)} %param.10) | copy-start | bytes 6291460
Sparse Core Ops, SparseCore 0:
  9.5 80.7 all-gather.2

commit v3 on v0

--- a/solution.py
+++ b/solution.py
@@ -67,10 +67,12 @@
             jnp.int32
         )
         ranking = jnp.sum((jnp.cumsum(matches, axis=0) - 1) * matches, axis=1)
-        slot_hits = (target[None, None, :] == jnp.arange(peer_count, dtype=jnp.int32)[:, None, None]) & (
-            ranking[None, None, :] == jnp.arange(slots_each, dtype=jnp.int32)[None, :, None]
-        )
-        tagged = jnp.sum(jnp.where(slot_hits, learner_slot[None, None, :] + 1, 0), axis=2)
+        parcel_rows = -(-(slots_each + 1) // 8) * 8
+        flat_slot = target * parcel_rows + ranking
+        slot_hits = flat_slot[None, :] == jnp.arange(peer_count * parcel_rows, dtype=jnp.int32)[:, None]
+        tagged = jnp.sum(jnp.where(slot_hits, learner_slot[None, :] + 1, 0), axis=1).reshape(
+            peer_count, parcel_rows
+        )[:, :slots_each]
         tag_row = jnp.concatenate(
             [
                 (tagged // 32).astype(jnp.bfloat16),
@@ -79,22 +81,22 @@
             ],
             axis=1,
         )
-        picked = jnp.einsum(
-            "psr,rf->psf",
-            slot_hits.astype(jnp.bfloat16),
-            rollout_rows,
-            preferred_element_type=jnp.float32,
-        ).astype(jnp.bfloat16)
-        payload = jnp.concatenate([picked, tag_row[:, None, :]], axis=1)
+        picked = jnp.dot(
+            slot_hits.astype(jnp.bfloat16), rollout_rows, preferred_element_type=jnp.float32
+        ).astype(jnp.bfloat16).reshape(peer_count, parcel_rows, width)
+        row_in_parcel = jnp.arange(parcel_rows, dtype=jnp.int32)[None, :, None]
+        payload = jnp.where(row_in_parcel == slots_each, tag_row[:, None, :], picked)
         arrived = lax.all_to_all(payload, SEQ, split_axis=0, concat_axis=0, tiled=True)
         tags = arrived[:, slots_each, : 2 * slots_each].astype(jnp.int32)
         labels = tags[:, :slots_each] * 32 + tags[:, slots_each:] - 1
+        labels = jnp.concatenate(
+            [labels, jnp.full((peer_count, parcel_rows - slots_each), -1, jnp.int32)], axis=1
+        ).reshape(peer_count * parcel_rows)
         row_numbers = jnp.arange(row_count, dtype=jnp.int32)
-        label_hits = labels[None, :, :] == row_numbers[:, None, None]
-        learner_part = jnp.einsum(
-            "rps,psf->rf",
+        label_hits = labels[None, :] == row_numbers[:, None]
+        learner_part = jnp.dot(
             label_hits.astype(jnp.bfloat16),
-            arrived[:, :slots_each, :],
+            arrived.reshape(peer_count * parcel_rows, width),
             preferred_element_type=jnp.float32,
         ).astype(jnp.bfloat16)
 

time: 272 us -> 270 us (level)
  no operation moved by 1% of the time
where the time goes in v3:
time: 270 us; the launch traced here: 269 us
  waiting for transfers between devices  139 us (51%)
  blocking collectives  44.7 us (17%)
  matrix products  35.1 us (13%)
  other arithmetic  18 us (7%)
  between operations  14.1 us (5%)
  starting transfers between devices  9.45 us (3%)
  local copies, waits for them, and re-layouts  9.43 us (3%)
    all_gather x1, waiting for transfers between devices, body(): own_weights = lax.all_gather(weights, CHIPS, axis=0, tiled=False)  77.5 us
    all_to_all x1, blocking collectives, body(): lax.all_to_all(payload, SEQ, split_axis=0, concat_axis=0, tiled=True)  44.7 us
    ppermute x3, waiting for transfers between devices, body(): lax.ppermute(own_sq, TP, [(t, (t + k) % tp_count) for t in range(tp_count)])  44.6 us
    dot_general x8, matrix products, project(): part = jnp.dot(cols, rows, preferred_element_type=jnp.float32)  23.6 us
    ppermute x1, waiting for transfers between devices, body(): far_b = lax.ppermute(from_right[:, half:], TP, to_left)  12.2 us
  transfers between devices with their start and end apart: 9, of which 6 were waited for; matrix products, arithmetic and copies ran while one was open for 13% of the time, Pallas kernels for 0%

profile of v3, /device:TPU:0, one launch (start us, length us, event | category | flops | bytes accessed | tf_op | source)
XLA Modules:
  0.0 269.4 jit_solution(9680738322875506854)
XLA Ops:
  6.5 2.1 pad_maximum_fusion.9
  8.7 0.7 fusion.84
  9.4 1.2 reduce-window.15
  10.6 0.2 slice_reduce_fusion
  10.8 0.1 fusion.76
  11.0 0.2 select_reduce_fusion
  11.2 0.1 reshape.275
  11.4 0.1 concatenate.58
  11.5 3.5 %convolution_convert_fusion = bf16[768,2048]{1,0:T(8,128)(2,1)} fusion(bf16[512,2048]{1,0:T(8,128)(2,1)S(1)} %copy-done, s32[512]{0:T(512)S(1)} %multiply_add_fusion), kind=kOutput, calls=%fused_computation.16 | convolution fusion | flops 1612578816 | bytes 5244928 | tf_op jit(solution)/shard_map/dot_general | solution.py:84
  15.0 77.5 %all-gather.3.cloned.1.call-done = bf16[4096,1280]{1,0:T(8,128)(2,1)} async-done(((bf16[256,1280]{1,0:T(8,128)(2,1)}), bf16[4096,1280]{1,0:T(8,128)(2,1)}) %all-gather.3.cloned.1.call-update) | async-done | bytes 10485776 | tf_op jit(solution)/shard_map/all_gather | solution.py:59
  92.5 2.2 broadcast_select_fusion
  94.7 44.7 %all_to_all.5 = bf16[32,24,2048]{2,1,0:T(8,128)(2,1)S(1)} all-to-all(bf16[32,24,2048]{2,1,0:T(8,128)(2,1)S(1)} %broadcast_select_fusion), channel_id=1, replica_groups=mesh['chips'=16,'core'=2,'tp'=4] {'chips','core'}, dimensions={0} | all-to-all | bytes 6291456 | tf_op jit(solution)/shard_map/all_to_all | solution.py:89
  139.6 0.1 eq.113
  139.7 3.2 %fusion.2 = (f32[512]{0:T(512)S(1)}, bf16[512,2048]{1,0:T(8,128)(2,1)}) fusion(bf16[768,2048]{1,0:T(8,128)(2,1)S(1)} %bitcast.105, s32[768]{0:T(1024)S(1)} %eq.113), kind=kOutput, calls=%fused_computation.7 | convolution fusion | flops 1615199744 | bytes 5248000 | tf_op jit(solution)/shard_map/dot_general | solution.py:97
  142.8 2.7 collective-permute-start.5
  145.6 0.1 add_select_fusion.4
  145.7 0.3 reduce-window.19
  146.0 0.1 slice.199
  146.1 0.1 slice_reduce_fusion.1
  146.2 0.1 fusion.85
  146.3 0.2 fusion.47
  146.5 1.0 multiply_cosine_fusion
  147.5 3.3 %collective-permute-start.2 = (f32[512]{0:T(512)S(1)}, f32[512]{0:T(512)S(1)}, u32[]{:S(2)}, u32[]{:S(2)}) collective-permute-start(f32[512]{0:T(512)S(1)} %get-tuple-element.65), channel_id=1, source_target_pairs={{0,3},{1,0},{2,1},{3,2},{4,7},{5,4},{6,5},{7,6},{8,11},{9,8},{10,9... | collective-permute-start | bytes 6152 | tf_op jit(solution)/shard_map/ppermute | solution.py:108
  150.8 40.6 %collective-permute-done.2 = f32[512]{0:T(512)S(1)} collective-permute-done((f32[512]{0:T(512)S(1)}, f32[512]{0:T(512)S(1)}, u32[]{:S(2)}, u32[]{:S(2)}) %collective-permute-start.2) | collective-permute-done | bytes 2080 | tf_op jit(solution)/shard_map/ppermute | solution.py:108
  191.4 1.1 collective-permute-start
  192.5 1.3 collective-permute-done.1
  193.8 2.7 %collective-permute-done = f32[512]{0:T(512)S(1)} collective-permute-done((f32[512]{0:T(512)S(1)}, f32[512]{0:T(512)S(1)}, u32[]{:S(2)}, u32[]{:S(2)}) %collective-permute-start) | collective-permute-done | bytes 2080 | tf_op jit(solution)/shard_map/ppermute | solution.py:108
  196.5 0.1 slice.235
  196.6 2.1 collective-permute-start.7
  198.7 1.3 slice.234
  200.0 0.3 collective-permute-start.6
  200.3 4.7 %fusion.4 = (bf16[512,2048]{1,0:T(8,128)(2,1)S(1)}, bf16[512,2048]{1,0:T(8,128)(2,1)S(1)}, bf16[512,2048]{1,0:T(8,128)(2,1)S(1)}) fusion(bf16[512,2048]{1,0:T(8,128)(2,1)} %get-tuple-element.66, f32[2048]{0:T(1024)S(1)} %get-tuple-element.55, f32[512]{0:T(512)S(1)} %add_rsqrt_fusion, f32[2048]{0:T(1024)S(1)} %get-tuple-element.56, ...), kind=kLoop, calls=%fused_computation.9 | loop fusion | flops 12582912 | bytes 12609536 | tf_op jit(solution)/shard_map/convert_element_type | solution.py:140
  205.0 1.3 fusion.110
  206.3 1.9 fusion.108
  208.2 12.2 %collective-permute-done.7 = bf16[512,1024]{1,0:T(8,128)(2,1)S(1)} collective-permute-done((bf16[512,1024]{1,0:T(8,128)(2,1)S(1)}, bf16[512,1024]{1,0:T(8,128)(2,1)S(1)}, u32[]{:S(2)}, u32[]{:S(2)}) %collective-permute-start.7) | collective-permute-done | bytes 1048608 | tf_op jit(solution)/shard_map/ppermute | solution.py:122
  220.5 4.2 %collective-permute-done.6 = bf16[512,1024]{1,0:T(8,128)(2,1)S(1)} collective-permute-done((bf16[512,1024]{1,0:T(8,128)(2,1)S(1)}, bf16[512,1024]{1,0:T(8,128)(2,1)S(1)}, u32[]{:S(2)}, u32[]{:S(2)}) %collective-permute-start.6) | collective-permute-done | bytes 1048608 | tf_op jit(solution)/shard_map/ppermute | solution.py:121
  224.7 0.2 pad_maximum_fusion
  224.9 0.5 multiply_convert_fusion
  225.5 0.1 fusion.107
  225.7 0.7 copy-done.8
  226.4 0.1 copy-done.9
  226.5 0.1 copy-done.10
  226.6 0.1 copy-done.11
  226.7 0.1 copy-done.12
  226.7 0.1 copy-done.13
  226.8 0.1 copy-done.14
  226.9 0.1 copy-done.15
  227.1 3.4 %fusion.15 = f32[512,1280]{1,0:T(8,128)S(1)} fusion(bf16[4,1024,1280]{2,1,0:T(8,128)(2,1)} %bitcast.110, s32[]{:T(128)S(6)} %select_n.152, pred[]{:T(512)S(6)} %eq.101, bf16[512,256]{1,0:T(8,128)(2,1)S(1)} %copy-done.9, bf16[512,256]{1,0:T(8,128)(2,1)S(1)} %copy-done.10, bf16[512,256]{1,0:T(8,128)(2,1)S(1)} %copy-done.11, ...), kind=kOutput, calls=%fused_computation.30 | convolution fusion | flops 1351090176 | bytes 7340037 | tf_op jit(solution)/shard_map/dot_general | solution.py:151
  230.6 3.5 %fusion.18 = f32[512,1280]{1,0:T(8,128)S(1)} fusion(bf16[4,1024,1280]{2,1,0:T(8,128)(2,1)} %bitcast.111, s32[]{:T(128)S(6)} %select_n.147, pred[]{:T(512)S(6)} %eq.101, bf16[512,256]{1,0:T(8,128)(2,1)S(1)} %copy-done.22, bf16[512,256]{1,0:T(8,128)(2,1)S(1)} %copy-done.21, bf16[512,256]{1,0:T(8,128)(2,1)S(1)} %copy-done.20, ...), kind=kOutput, calls=%fused_computation.33 | convolution fusion | flops 1351090176 | bytes 7340037 | tf_op jit(solution)/shard_map/dot_general | solution.py:151
  234.3 1.6 fusion.21
  235.9 1.6 fusion.12
  237.4 3.3 %convolution_add_fusion.1 = f32[512,1280]{1,0:T(8,128)S(1)} fusion(f32[512,1280]{1,0:T(8,128)S(1)} %fusion.15, bf16[4,1024,1280]{2,1,0:T(8,128)(2,1)} %bitcast.9, s32[]{:T(128)S(6)} %select_n.152, pred[]{:T(512)S(6)} %eq.101, bf16[512,256]{1,0:T(8,128)(2,1)S(1)} %copy-done.9, bf16[512,256]{1,0:T(8,128)(2,1)S(1)} %copy-done.10, ...), kind=kOutput, calls=%fused_computation.18 | convolution fusion | flops 1351745536 | bytes 9961477 | tf_op jit(solution)/shard_map/dot_general | solution.py:151
  240.7 3.3 %convolution_add_fusion.2 = f32[512,1280]{1,0:T(8,128)S(1)} fusion(f32[512,1280]{1,0:T(8,128)S(1)} %fusion.18, bf16[4,1024,1280]{2,1,0:T(8,128)(2,1)} %bitcast.9, s32[]{:T(128)S(6)} %select_n.147, pred[]{:T(512)S(6)} %eq.101, bf16[512,256]{1,0:T(8,128)(2,1)S(1)} %copy-done.22, bf16[512,256]{1,0:T(8,128)(2,1)S(1)} %copy-done.21, ...), kind=kOutput, calls=%fused_computation.19 | convolution fusion | flops 1351745536 | bytes 9961477 | tf_op jit(solution)/shard_map/dot_general | solution.py:151
  244.0 3.6 %fusion.10 = f32[512,1280]{1,0:T(8,128)S(1)} fusion(f32[512,1280]{1,0:T(8,128)S(1)} %convolution_add_fusion.1, f32[512,1280]{1,0:T(8,128)S(1)} %convolution_add_fusion.2, f32[512,1280]{1,0:T(8,128)S(1)} %fusion.21, bf16[4,1024,1280]{2,1,0:T(8,128)(2,1)} %bitcast.9, s32[]{:T(128)S(6)} %select_n.142, pred[]{:T(512)S(6)} %eq.101, ...), kind=kOutput, calls=%fused_computation.23 | convolution fusion | flops 1353056256 | bytes 15204357 | tf_op jit(solution)/shard_map/dot_general | solution.py:151
  247.6 3.3 %fusion.9 = f32[512,1280]{1,0:T(8,128)S(1)} fusion(f32[512,1280]{1,0:T(8,128)S(1)} %fusion.10, f32[512,1280]{1,0:T(8,128)S(1)} %fusion.12, bf16[4,1024,1280]{2,1,0:T(8,128)(2,1)} %bitcast.9, s32[]{:T(128)S(6)} %select_n.158, pred[]{:T(512)S(6)} %eq.117, bf16[512,256]{1,0:T(8,128)(2,1)S(1)} %get-tuple-element.22, ...), kind=kOutput, calls=%fused_computation.22 | convolution fusion | flops 1352400896 | bytes 12582917 | tf_op jit(solution)/shard_map/dot_general | solution.py:151
  251.0 0.3 fusion.31
  251.3 0.5 copy.52
  251.8 0.7 fusion.106
  252.5 1.2 fusion.74
  253.7 0.8 subtract_convert_fusion
  254.5 2.2 fusion.1
  256.8 1.7 fusion
  258.5 2.7 fusion.32
  261.2 1.3 copy.44
  (84 shorter events, 0.5 us)
Async XLA Ops:
  6.5 5.0 %copy-start = (bf16[512,2048]{1,0:T(8,128)(2,1)S(1)}, bf16[512,2048]{1,0:T(8,128)(2,1)}, u32[]{:S(2)}) copy-start(bf16[512,2048]{1,0:T(8,128)(2,1)} %param.10) | copy-start | bytes 6291460
  6.5 85.9 %all-gather.3.cloned.1.call-start = ((), (), s32[]{:S(2)}) async-start(), calls=%async_computation.1 | async-start | bytes 11141120 | tf_op jit(solution)/shard_map/all_gather | solution.py:59
  92.5 144.9 %collective-permute-start.3 = (bf16[16,256,1280]{2,1,0:T(8,128)(2,1)}, bf16[16,256,1280]{2,1,0:T(8,128)(2,1)}, u32[]{:S(2)}, u32[]{:S(2)}) collective-permute-start(bf16[16,256,1280]{2,1,0:T(8,128)(2,1)} %bitcast.109), channel_id=1, source_target_pairs={{0,4},{4,0},{1,5},{5,1},{2,6},{6,2},{3,7},{7,3},{8,12},{12,8},{9,1... | collective-permute-start | bytes 31457288 | tf_op jit(solution)/shard_map/ppermute | solution.py:60
  139.6 5.9 %copy-start.24 = (s32[512]{0:T(512)S(1)}, s32[512]{0:T(512)}, u32[]{:S(2)}) copy-start(s32[512]{0:T(512)} %param.12) | copy-start | bytes 6148
  139.7 52.8 %copy-start.25 = (f32[8192]{0:T(1024)S(1)}, f32[8192]{0:T(1024)}, u32[]{:S(2)}) copy-start(f32[8192]{0:T(1024)} %param.13) | copy-start | bytes 98308
  142.8 53.7 %collective-permute-start.5 = (bf16[512,2048]{1,0:T(8,128)(2,1)}, bf16[512,2048]{1,0:T(8,128)(2,1)S(1)}, u32[]{:S(2)}, u32[]{:S(2)}) collective-permute-start(bf16[512,2048]{1,0:T(8,128)(2,1)} %get-tuple-element.66), channel_id=1, source_target_pairs={{0,3},{1,0},{2,1},{3,2},{4,7},{5,4},{6,5},{7,6},{8,11},{9,8},{10,9... | collective-permute-start | bytes 6291464 | tf_op jit(solution)/shard_map/ppermute | solution.py:120
  145.5 53.2 %collective-permute-start.4 = (bf16[512,2048]{1,0:T(8,128)(2,1)}, bf16[512,2048]{1,0:T(8,128)(2,1)}, u32[]{:S(2)}, u32[]{:S(2)}) collective-permute-start(bf16[512,2048]{1,0:T(8,128)(2,1)} %get-tuple-element.66), channel_id=1, source_target_pairs={{0,1},{1,2},{2,3},{3,0},{4,5},{5,6},{6,7},{7,4},{8,9},{9,10},{10,1... | collective-permute-start | bytes 6291464 | tf_op jit(solution)/shard_map/ppermute | solution.py:119
  147.5 43.9 %collective-permute-start.2 = (f32[512]{0:T(512)S(1)}, f32[512]{0:T(512)S(1)}, u32[]{:S(2)}, u32[]{:S(2)}) collective-permute-start(f32[512]{0:T(512)S(1)} %get-tuple-element.65), channel_id=1, source_target_pairs={{0,3},{1,0},{2,1},{3,2},{4,7},{5,4},{6,5},{7,6},{8,11},{9,8},{10,9... | collective-permute-start | bytes 6152 | tf_op jit(solution)/shard_map/ppermute | solution.py:108
  150.8 43.0 %collective-permute-start.1 = (f32[512]{0:T(512)S(1)}, f32[512]{0:T(512)S(1)}, u32[]{:S(2)}, u32[]{:S(2)}) collective-permute-start(f32[512]{0:T(512)S(1)} %get-tuple-element.65), channel_id=1, source_target_pairs={{0,2},{1,3},{2,0},{3,1},{4,6},{5,7},{6,4},{7,5},{8,10},{9,11},{10,... | collective-permute-start | bytes 6152 | tf_op jit(solution)/shard_map/ppermute | solution.py:108
  191.4 5.1 %collective-permute-start = (f32[512]{0:T(512)S(1)}, f32[512]{0:T(512)S(1)}, u32[]{:S(2)}, u32[]{:S(2)}) collective-permute-start(f32[512]{0:T(512)S(1)} %get-tuple-element.65), channel_id=1, source_target_pairs={{0,1},{1,2},{2,3},{3,0},{4,5},{5,6},{6,7},{7,4},{8,9},{9,10},{10,1... | collective-permute-start | bytes 6152 | tf_op jit(solution)/shard_map/ppermute | solution.py:108
  196.6 23.8 %collective-permute-start.7 = (bf16[512,1024]{1,0:T(8,128)(2,1)S(1)}, bf16[512,1024]{1,0:T(8,128)(2,1)S(1)}, u32[]{:S(2)}, u32[]{:S(2)}) collective-permute-start(bf16[512,1024]{1,0:T(8,128)(2,1)S(1)} %slice.235), channel_id=1, source_target_pairs={{0,3},{1,0},{2,1},{3,2},{4,7},{5,4},{6,5},{7,6},{8,11},{9,8},{10,9... | collective-permute-start | bytes 3145736 | tf_op jit(solution)/shard_map/ppermute | solution.py:122
  200.0 24.6 %collective-permute-start.6 = (bf16[512,1024]{1,0:T(8,128)(2,1)S(1)}, bf16[512,1024]{1,0:T(8,128)(2,1)S(1)}, u32[]{:S(2)}, u32[]{:S(2)}) collective-permute-start(bf16[512,1024]{1,0:T(8,128)(2,1)S(1)} %slice.234), channel_id=1, source_target_pairs={{0,1},{1,2},{2,3},{3,0},{4,5},{5,6},{6,7},{7,4},{8,9},{9,10},{10,1... | collective-permute-start | bytes 3145736 | tf_op jit(solution)/shard_map/ppermute | solution.py:121
  225.5 1.0 copy-start.8
  225.5 1.0 copy-start.9
  225.5 1.1 copy-start.10
  225.5 1.2 copy-start.11
  225.5 1.2 copy-start.12
  225.5 1.3 copy-start.13
  225.5 1.4 copy-start.14
  225.5 1.4 copy-start.15
  227.0 3.5 %copy-start.16 = (bf16[512,256]{1,0:T(8,128)(2,1)S(1)}, bf16[512,256]{1,0:T(8,128)(2,1)}, u32[]{:S(2)}) copy-start(bf16[512,256]{1,0:T(8,128)(2,1)} %get-tuple-element.69) | copy-start | bytes 786436
  227.0 3.5 %copy-start.17 = (bf16[512,256]{1,0:T(8,128)(2,1)S(1)}, bf16[512,256]{1,0:T(8,128)(2,1)}, u32[]{:S(2)}) copy-start(bf16[512,256]{1,0:T(8,128)(2,1)} %get-tuple-element.70) | copy-start | bytes 786436
  227.0 3.5 %copy-start.18 = (bf16[512,256]{1,0:T(8,128)(2,1)S(1)}, bf16[512,256]{1,0:T(8,128)(2,1)}, u32[]{:S(2)}) copy-start(bf16[512,256]{1,0:T(8,128)(2,1)} %get-tuple-element.71) | copy-start | bytes 786436
  227.0 3.5 %copy-start.19 = (bf16[512,256]{1,0:T(8,128)(2,1)S(1)}, bf16[512,256]{1,0:T(8,128)(2,1)}, u32[]{:S(2)}) copy-start(bf16[512,256]{1,0:T(8,128)(2,1)} %get-tuple-element.72) | copy-start | bytes 786436
  227.0 3.5 %copy-start.20 = (bf16[512,256]{1,0:T(8,128)(2,1)S(1)}, bf16[512,256]{1,0:T(8,128)(2,1)}, u32[]{:S(2)}) copy-start(bf16[512,256]{1,0:T(8,128)(2,1)} %get-tuple-element.73) | copy-start | bytes 786436
  227.0 3.5 %copy-start.21 = (bf16[512,256]{1,0:T(8,128)(2,1)S(1)}, bf16[512,256]{1,0:T(8,128)(2,1)}, u32[]{:S(2)}) copy-start(bf16[512,256]{1,0:T(8,128)(2,1)} %get-tuple-element.74) | copy-start | bytes 786436
  227.0 3.5 %copy-start.22 = (bf16[512,256]{1,0:T(8,128)(2,1)S(1)}, bf16[512,256]{1,0:T(8,128)(2,1)}, u32[]{:S(2)}) copy-start(bf16[512,256]{1,0:T(8,128)(2,1)} %get-tuple-element.75) | copy-start | bytes 786436
  227.0 3.5 %copy-start.23 = (bf16[512,256]{1,0:T(8,128)(2,1)S(1)}, bf16[512,256]{1,0:T(8,128)(2,1)}, u32[]{:S(2)}) copy-start(bf16[512,256]{1,0:T(8,128)(2,1)} %get-tuple-element.76) | copy-start | bytes 786436
  227.0 7.1 %slice-start = ((s8[10485760]{0:T(1024)(128)(4,1)}), s8[4194304]{0:T(1024)(128)(4,1)S(1)}, s32[]{:S(2)}) async-start(s8[10485760]{0:T(1024)(128)(4,1)} %bitcast.112), calls=%async_computation.2 | async-start | bytes 8388608
  227.0 7.1 %slice-start.1 = ((s8[10485760]{0:T(1024)(128)(4,1)}), s8[4194304]{0:T(1024)(128)(4,1)S(1)}, s32[]{:S(2)}) async-start(s8[10485760]{0:T(1024)(128)(4,1)} %bitcast.112), calls=%async_computation.3 | async-start | bytes 8388608
  230.6 3.6 %copy-start.2 = (bf16[512,256]{1,0:T(8,128)(2,1)S(1)}, bf16[512,256]{1,0:T(8,128)(2,1)}, u32[]{:S(2)}) copy-start(bf16[512,256]{1,0:T(8,128)(2,1)} %get-tuple-element.31) | copy-start | bytes 786436
  230.6 3.6 %copy-start.3 = (bf16[512,256]{1,0:T(8,128)(2,1)S(1)}, bf16[512,256]{1,0:T(8,128)(2,1)}, u32[]{:S(2)}) copy-start(bf16[512,256]{1,0:T(8,128)(2,1)} %get-tuple-element.32) | copy-start | bytes 786436
  230.6 3.6 %copy-start.4 = (bf16[512,256]{1,0:T(8,128)(2,1)S(1)}, bf16[512,256]{1,0:T(8,128)(2,1)}, u32[]{:S(2)}) copy-start(bf16[512,256]{1,0:T(8,128)(2,1)} %get-tuple-element.33) | copy-start | bytes 786436
  230.6 3.6 %copy-start.5 = (bf16[512,256]{1,0:T(8,128)(2,1)S(1)}, bf16[512,256]{1,0:T(8,128)(2,1)}, u32[]{:S(2)}) copy-start(bf16[512,256]{1,0:T(8,128)(2,1)} %get-tuple-element.34) | copy-start | bytes 786436
  230.6 3.6 %copy-start.6 = (bf16[512,256]{1,0:T(8,128)(2,1)S(1)}, bf16[512,256]{1,0:T(8,128)(2,1)}, u32[]{:S(2)}) copy-start(bf16[512,256]{1,0:T(8,128)(2,1)} %get-tuple-element.35) | copy-start | bytes 786436
  230.6 3.6 %copy-start.7 = (bf16[512,256]{1,0:T(8,128)(2,1)S(1)}, bf16[512,256]{1,0:T(8,128)(2,1)}, u32[]{:S(2)}) copy-start(bf16[512,256]{1,0:T(8,128)(2,1)} %get-tuple-element.36) | copy-start | bytes 786436
  230.6 3.6 %slice-start.2 = ((s8[10485760]{0:T(1024)(128)(4,1)}), s8[2097152]{0:T(1024)(128)(4,1)S(1)}, s32[]{:S(2)}) async-start(s8[10485760]{0:T(1024)(128)(4,1)} %bitcast.112), calls=%async_computation.4 | async-start | bytes 4194304
  247.6 3.3 %copy-start.26 = (f32[1024]{0:T(1024)S(1)}, f32[1024]{0:T(1024)}, u32[]{:S(2)}) copy-start(f32[1024]{0:T(1024)} %param.17) | copy-start | bytes 12292
  251.8 0.7 copy-start.27
  256.7 1.8 copy-start.28
  258.5 4.0 %copy-start.1 = (bf16[512,2048]{1,0:T(8,128)(2,1)S(1)}, bf16[512,2048]{1,0:T(8,128)(2,1)}, u32[]{:S(2)}) copy-start(bf16[512,2048]{1,0:T(8,128)(2,1)} %param.10) | copy-start | bytes 6291460
Sparse Core Ops, SparseCore 0:
  9.5 82.9 all-gather.2

commit v4 on v3

--- a/solution.py
+++ b/solution.py
@@ -104,13 +104,7 @@
         core_index = lax.axis_index(CORE)
         wide = learner_part.astype(jnp.float32)
         own_sq = jnp.sum(wide * wide, axis=-1)
-        others = [
-            lax.ppermute(own_sq, TP, [(t, (t + k) % tp_count) for t in range(tp_count)])
-            for k in range(1, tp_count)
-        ]
-        total_sq = own_sq
-        for other in others:
-            total_sq = total_sq + other
+        total_sq = lax.psum(own_sq, TP)
         scale = lax.rsqrt(total_sq / (width * tp_count) + EPS)[:, None]
 
         to_right = [(t, (t + 1) % tp_count) for t in range(tp_count)]

time: 270 us -> 268 us (level)
  the two profiles are of different devices: /device:TPU:0 before, /device:TPU:49 now
where the time goes in v4:
time: 268 us; the launch traced here: 264 us
  blocking collectives  91.5 us (34%)
  waiting for transfers between devices  90.3 us (34%)
  matrix products  35.1 us (13%)
  other arithmetic  18 us (7%)
  between operations  14.2 us (5%)
  local copies, waits for them, and re-layouts  9.5 us (4%)
  starting transfers between devices  5.02 us (2%)
    all_gather x1, waiting for transfers between devices, body(): own_weights = lax.all_gather(weights, CHIPS, axis=0, tiled=False)  75.3 us
    psum x1, blocking collectives, body(): total_sq = lax.psum(own_sq, TP)  47.9 us
    all_to_all x1, blocking collectives, body(): lax.all_to_all(payload, SEQ, split_axis=0, concat_axis=0, tiled=True)  43.6 us
    dot_general x8, matrix products, project(): part = jnp.dot(cols, rows, preferred_element_type=jnp.float32)  23.6 us
    ppermute x1, waiting for transfers between devices, body(): far_b = lax.ppermute(from_right[:, half:], TP, to_left)  12.2 us
  transfers between devices with their start and end apart: 6, of which 3 were waited for; matrix products, arithmetic and copies ran while one was open for 13% of the time, Pallas kernels for 0%

profile of v4, /device:TPU:49, one launch (start us, length us, event | category | flops | bytes accessed | tf_op | source)
XLA Modules:
  0.0 263.5 jit_solution(18025086129783894911)
XLA Ops:
  6.5 2.1 pad_maximum_fusion.9
  8.7 0.0 all-gather.3.cloned.1.call-update
  8.7 0.7 fusion.84
  9.4 1.2 reduce-window.15
  10.6 0.2 slice_reduce_fusion
  10.8 0.1 fusion.76
  11.0 0.2 select_reduce_fusion
  11.2 0.1 reshape.275
  11.4 0.1 concatenate.58
  11.5 3.5 %convolution_convert_fusion = bf16[768,2048]{1,0:T(8,128)(2,1)} fusion(bf16[512,2048]{1,0:T(8,128)(2,1)S(1)} %copy-done, s32[512]{0:T(512)S(1)} %multiply_add_fusion), kind=kOutput, calls=%fused_computation.16 | convolution fusion | flops 1612578816 | bytes 5244928 | tf_op jit(solution)/shard_map/dot_general | solution.py:84
  15.0 75.3 %all-gather.3.cloned.1.call-done = bf16[4096,1280]{1,0:T(8,128)(2,1)} async-done(((bf16[256,1280]{1,0:T(8,128)(2,1)}), bf16[4096,1280]{1,0:T(8,128)(2,1)}) %all-gather.3.cloned.1.call-update) | async-done | bytes 10485776 | tf_op jit(solution)/shard_map/all_gather | solution.py:59
  90.3 0.8 collective-permute-start
  91.1 2.2 broadcast_select_fusion
  93.3 43.6 %all_to_all.5 = bf16[32,24,2048]{2,1,0:T(8,128)(2,1)S(1)} all-to-all(bf16[32,24,2048]{2,1,0:T(8,128)(2,1)S(1)} %broadcast_select_fusion), channel_id=1, replica_groups=mesh['chips'=16,'core'=2,'tp'=4] {'chips','core'}, dimensions={0} | all-to-all | bytes 6291456 | tf_op jit(solution)/shard_map/all_to_all | solution.py:89
  136.9 0.1 fusion.80
  137.0 0.1 eq.113
  137.1 3.2 %fusion.2 = (f32[512]{0:T(512)S(1)}, bf16[512,2048]{1,0:T(8,128)(2,1)}) fusion(bf16[768,2048]{1,0:T(8,128)(2,1)S(1)} %bitcast.105, s32[768]{0:T(1024)S(1)} %eq.113), kind=kOutput, calls=%fused_computation.7 | convolution fusion | flops 1615199744 | bytes 5248000 | tf_op jit(solution)/shard_map/dot_general | solution.py:97
  140.3 2.4 collective-permute-start.2
  142.7 0.1 slice_compare_fusion.1
  142.8 0.1 add_select_fusion.4
  142.8 0.3 reduce-window.19
  143.2 0.1 slice.199
  143.3 0.1 slice_reduce_fusion.1
  143.4 0.1 fusion.85
  143.5 0.2 fusion.47
  143.7 1.0 multiply_cosine_fusion
  144.7 47.9 %psum.7 = f32[512]{0:T(512)S(1)} all-reduce(f32[512]{0:T(512)S(1)} %get-tuple-element.65), channel_id=1, replica_groups=mesh['chips'=16,'core'=2,'tp'=4] {'tp'}, use_global_device_ids=true, to_apply=%region_5.6 | all-reduce | flops 512 | bytes 4096 | tf_op jit(solution)/shard_map/psum | solution.py:107
  192.6 0.1 slice.235
  192.8 0.1 collective-permute-start.4
  192.8 1.3 slice.234
  194.1 1.7 collective-permute-start.3
  195.8 4.7 %fusion.4 = (bf16[512,2048]{1,0:T(8,128)(2,1)S(1)}, bf16[512,2048]{1,0:T(8,128)(2,1)S(1)}, bf16[512,2048]{1,0:T(8,128)(2,1)S(1)}) fusion(bf16[512,2048]{1,0:T(8,128)(2,1)} %get-tuple-element.66, f32[2048]{0:T(1024)S(1)} %get-tuple-element.55, f32[512]{0:T(512)S(1)} %add_rsqrt_fusion, f32[2048]{0:T(1024)S(1)} %get-tuple-element.56, ...), kind=kLoop, calls=%fused_computation.9 | loop fusion | flops 12582912 | bytes 12609536 | tf_op jit(solution)/shard_map/convert_element_type | solution.py:134
  200.5 1.3 fusion.110
  201.9 2.0 fusion.108
  203.8 12.2 %collective-permute-done.4 = bf16[512,1024]{1,0:T(8,128)(2,1)S(1)} collective-permute-done((bf16[512,1024]{1,0:T(8,128)(2,1)S(1)}, bf16[512,1024]{1,0:T(8,128)(2,1)S(1)}, u32[]{:S(2)}, u32[]{:S(2)}) %collective-permute-start.4) | collective-permute-done | bytes 1048608 | tf_op jit(solution)/shard_map/ppermute | solution.py:116
  216.0 2.8 %collective-permute-done.3 = bf16[512,1024]{1,0:T(8,128)(2,1)S(1)} collective-permute-done((bf16[512,1024]{1,0:T(8,128)(2,1)S(1)}, bf16[512,1024]{1,0:T(8,128)(2,1)S(1)}, u32[]{:S(2)}, u32[]{:S(2)}) %collective-permute-start.3) | collective-permute-done | bytes 1048608 | tf_op jit(solution)/shard_map/ppermute | solution.py:115
  218.8 0.2 pad_maximum_fusion
  219.1 0.5 multiply_convert_fusion
  219.7 0.1 fusion.107
  219.8 0.7 copy-done.8
  220.6 0.1 copy-done.9
  220.7 0.1 copy-done.10
  220.7 0.1 copy-done.11
  220.8 0.1 copy-done.12
  220.9 0.1 copy-done.13
  221.0 0.1 copy-done.14
  221.1 0.1 copy-done.15
  221.2 3.4 %fusion.15 = f32[512,1280]{1,0:T(8,128)S(1)} fusion(bf16[4,1024,1280]{2,1,0:T(8,128)(2,1)} %bitcast.110, s32[]{:T(128)S(6)} %select_n.152, pred[]{:T(512)S(6)} %eq.101, bf16[512,256]{1,0:T(8,128)(2,1)S(1)} %copy-done.9, bf16[512,256]{1,0:T(8,128)(2,1)S(1)} %copy-done.10, bf16[512,256]{1,0:T(8,128)(2,1)S(1)} %copy-done.11, ...), kind=kOutput, calls=%fused_computation.30 | convolution fusion | flops 1351090176 | bytes 7340037 | tf_op jit(solution)/shard_map/dot_general | solution.py:145
  224.8 3.5 %fusion.18 = f32[512,1280]{1,0:T(8,128)S(1)} fusion(bf16[4,1024,1280]{2,1,0:T(8,128)(2,1)} %bitcast.111, s32[]{:T(128)S(6)} %select_n.147, pred[]{:T(512)S(6)} %eq.101, bf16[512,256]{1,0:T(8,128)(2,1)S(1)} %copy-done.22, bf16[512,256]{1,0:T(8,128)(2,1)S(1)} %copy-done.21, bf16[512,256]{1,0:T(8,128)(2,1)S(1)} %copy-done.20, ...), kind=kOutput, calls=%fused_computation.33 | convolution fusion | flops 1351090176 | bytes 7340037 | tf_op jit(solution)/shard_map/dot_general | solution.py:145
  228.4 1.6 fusion.21
  230.0 1.6 fusion.12
  231.6 3.3 %convolution_add_fusion.1 = f32[512,1280]{1,0:T(8,128)S(1)} fusion(f32[512,1280]{1,0:T(8,128)S(1)} %fusion.15, bf16[4,1024,1280]{2,1,0:T(8,128)(2,1)} %bitcast.9, s32[]{:T(128)S(6)} %select_n.152, pred[]{:T(512)S(6)} %eq.101, bf16[512,256]{1,0:T(8,128)(2,1)S(1)} %copy-done.9, bf16[512,256]{1,0:T(8,128)(2,1)S(1)} %copy-done.10, ...), kind=kOutput, calls=%fused_computation.18 | convolution fusion | flops 1351745536 | bytes 9961477 | tf_op jit(solution)/shard_map/dot_general | solution.py:145
  234.9 3.3 %convolution_add_fusion.2 = f32[512,1280]{1,0:T(8,128)S(1)} fusion(f32[512,1280]{1,0:T(8,128)S(1)} %fusion.18, bf16[4,1024,1280]{2,1,0:T(8,128)(2,1)} %bitcast.9, s32[]{:T(128)S(6)} %select_n.147, pred[]{:T(512)S(6)} %eq.101, bf16[512,256]{1,0:T(8,128)(2,1)S(1)} %copy-done.22, bf16[512,256]{1,0:T(8,128)(2,1)S(1)} %copy-done.21, ...), kind=kOutput, calls=%fused_computation.19 | convolution fusion | flops 1351745536 | bytes 9961477 | tf_op jit(solution)/shard_map/dot_general | solution.py:145
  238.2 3.6 %fusion.10 = f32[512,1280]{1,0:T(8,128)S(1)} fusion(f32[512,1280]{1,0:T(8,128)S(1)} %convolution_add_fusion.1, f32[512,1280]{1,0:T(8,128)S(1)} %convolution_add_fusion.2, f32[512,1280]{1,0:T(8,128)S(1)} %fusion.21, bf16[4,1024,1280]{2,1,0:T(8,128)(2,1)} %bitcast.9, s32[]{:T(128)S(6)} %select_n.142, pred[]{:T(512)S(6)} %eq.101, ...), kind=kOutput, calls=%fused_computation.23 | convolution fusion | flops 1353056256 | bytes 15204357 | tf_op jit(solution)/shard_map/dot_general | solution.py:145
  241.8 3.3 %fusion.9 = f32[512,1280]{1,0:T(8,128)S(1)} fusion(f32[512,1280]{1,0:T(8,128)S(1)} %fusion.10, f32[512,1280]{1,0:T(8,128)S(1)} %fusion.12, bf16[4,1024,1280]{2,1,0:T(8,128)(2,1)} %bitcast.9, s32[]{:T(128)S(6)} %select_n.158, pred[]{:T(512)S(6)} %eq.117, bf16[512,256]{1,0:T(8,128)(2,1)S(1)} %get-tuple-element.22, ...), kind=kOutput, calls=%fused_computation.22 | convolution fusion | flops 1352400896 | bytes 12582917 | tf_op jit(solution)/shard_map/dot_general | solution.py:145
  245.1 0.3 fusion.31
  245.4 0.5 copy.52
  245.9 0.7 fusion.106
  246.6 1.2 fusion.74
  247.9 0.8 subtract_convert_fusion
  248.7 2.2 fusion.1
  250.9 1.7 fusion
  252.7 2.7 %fusion.32 = bf16[128,8,512]{2,0,1:T(8,128)(2,1)S(1)} fusion(f32[8,512]{1,0:T(8,128)S(1)} %fusion, f32[8,512]{1,0:T(8,128)S(1)} %get-tuple-element.67, f32[512,512,8]{1,0,2:T(8,128)S(1)} %get-tuple-element.68, pred[512,512]{0,1:T(8,128)(4,1)S(1)} %fusion.47, f32[512,1280]{1,0:T(8,128)S(1)} %fusion.9, f32[128]{0:T(128)S(1)} %copy-done.28), kind=kOutput, calls=%fused_computation.54 | convolution fusion | flops 548012032 | bytes 9994752 | tf_op jit(solution)/shard_map/kgqp,pkd->qkgd/dot_general | solution.py:187
  255.3 1.3 copy.44
  (79 shorter events, 0.4 us)
Async XLA Ops:
  6.5 5.0 %copy-start = (bf16[512,2048]{1,0:T(8,128)(2,1)S(1)}, bf16[512,2048]{1,0:T(8,128)(2,1)}, u32[]{:S(2)}) copy-start(bf16[512,2048]{1,0:T(8,128)(2,1)} %param.10) | copy-start | bytes 6291460
  6.5 83.7 %all-gather.3.cloned.1.call-start = ((), (), s32[]{:S(2)}) async-start(), calls=%async_computation.1 | async-start | bytes 11141120 | tf_op jit(solution)/shard_map/all_gather | solution.py:59
  90.3 141.3 %collective-permute-start = (bf16[16,256,1280]{2,1,0:T(8,128)(2,1)}, bf16[16,256,1280]{2,1,0:T(8,128)(2,1)}, u32[]{:S(2)}, u32[]{:S(2)}) collective-permute-start(bf16[16,256,1280]{2,1,0:T(8,128)(2,1)} %bitcast.109), channel_id=1, source_target_pairs={{0,4},{4,0},{1,5},{5,1},{2,6},{6,2},{3,7},{7,3},{8,12},{12,8},{9,1... | collective-permute-start | bytes 31457288 | tf_op jit(solution)/shard_map/ppermute | solution.py:60
  137.1 5.6 %copy-start.24 = (s32[512]{0:T(512)S(1)}, s32[512]{0:T(512)}, u32[]{:S(2)}) copy-start(s32[512]{0:T(512)} %param.12) | copy-start | bytes 6148
  137.1 6.3 %copy-start.25 = (f32[8192]{0:T(1024)S(1)}, f32[8192]{0:T(1024)}, u32[]{:S(2)}) copy-start(f32[8192]{0:T(1024)} %param.13) | copy-start | bytes 98308
  140.3 52.4 %collective-permute-start.2 = (bf16[512,2048]{1,0:T(8,128)(2,1)}, bf16[512,2048]{1,0:T(8,128)(2,1)S(1)}, u32[]{:S(2)}, u32[]{:S(2)}) collective-permute-start(bf16[512,2048]{1,0:T(8,128)(2,1)} %get-tuple-element.66), channel_id=1, source_target_pairs={{0,3},{1,0},{2,1},{3,2},{4,7},{5,4},{6,5},{7,6},{8,11},{9,8},{10,9... | collective-permute-start | bytes 6291464 | tf_op jit(solution)/shard_map/ppermute | solution.py:114
  142.7 50.1 %collective-permute-start.1 = (bf16[512,2048]{1,0:T(8,128)(2,1)}, bf16[512,2048]{1,0:T(8,128)(2,1)}, u32[]{:S(2)}, u32[]{:S(2)}) collective-permute-start(bf16[512,2048]{1,0:T(8,128)(2,1)} %get-tuple-element.66), channel_id=1, source_target_pairs={{0,1},{1,2},{2,3},{3,0},{4,5},{5,6},{6,7},{7,4},{8,9},{9,10},{10,1... | collective-permute-start | bytes 6291464 | tf_op jit(solution)/shard_map/ppermute | solution.py:113
  192.8 23.3 %collective-permute-start.4 = (bf16[512,1024]{1,0:T(8,128)(2,1)S(1)}, bf16[512,1024]{1,0:T(8,128)(2,1)S(1)}, u32[]{:S(2)}, u32[]{:S(2)}) collective-permute-start(bf16[512,1024]{1,0:T(8,128)(2,1)S(1)} %slice.235), channel_id=1, source_target_pairs={{0,3},{1,0},{2,1},{3,2},{4,7},{5,4},{6,5},{7,6},{8,11},{9,8},{10,9... | collective-permute-start | bytes 3145736 | tf_op jit(solution)/shard_map/ppermute | solution.py:116
  194.1 24.7 %collective-permute-start.3 = (bf16[512,1024]{1,0:T(8,128)(2,1)S(1)}, bf16[512,1024]{1,0:T(8,128)(2,1)S(1)}, u32[]{:S(2)}, u32[]{:S(2)}) collective-permute-start(bf16[512,1024]{1,0:T(8,128)(2,1)S(1)} %slice.234), channel_id=1, source_target_pairs={{0,1},{1,2},{2,3},{3,0},{4,5},{5,6},{6,7},{7,4},{8,9},{9,10},{10,1... | collective-permute-start | bytes 3145736 | tf_op jit(solution)/shard_map/ppermute | solution.py:115
  219.6 1.0 copy-start.8
  219.6 1.0 copy-start.9
  219.6 1.1 copy-start.10
  219.7 1.2 copy-start.11
  219.7 1.2 copy-start.12
  219.7 1.3 copy-start.13
  219.7 1.4 copy-start.14
  219.7 1.4 copy-start.15
  221.1 3.5 %copy-start.16 = (bf16[512,256]{1,0:T(8,128)(2,1)S(1)}, bf16[512,256]{1,0:T(8,128)(2,1)}, u32[]{:S(2)}) copy-start(bf16[512,256]{1,0:T(8,128)(2,1)} %get-tuple-element.69) | copy-start | bytes 786436
  221.1 3.5 %copy-start.17 = (bf16[512,256]{1,0:T(8,128)(2,1)S(1)}, bf16[512,256]{1,0:T(8,128)(2,1)}, u32[]{:S(2)}) copy-start(bf16[512,256]{1,0:T(8,128)(2,1)} %get-tuple-element.70) | copy-start | bytes 786436
  221.1 3.5 %copy-start.18 = (bf16[512,256]{1,0:T(8,128)(2,1)S(1)}, bf16[512,256]{1,0:T(8,128)(2,1)}, u32[]{:S(2)}) copy-start(bf16[512,256]{1,0:T(8,128)(2,1)} %get-tuple-element.71) | copy-start | bytes 786436
  221.1 3.5 %copy-start.19 = (bf16[512,256]{1,0:T(8,128)(2,1)S(1)}, bf16[512,256]{1,0:T(8,128)(2,1)}, u32[]{:S(2)}) copy-start(bf16[512,256]{1,0:T(8,128)(2,1)} %get-tuple-element.72) | copy-start | bytes 786436
  221.1 3.5 %copy-start.20 = (bf16[512,256]{1,0:T(8,128)(2,1)S(1)}, bf16[512,256]{1,0:T(8,128)(2,1)}, u32[]{:S(2)}) copy-start(bf16[512,256]{1,0:T(8,128)(2,1)} %get-tuple-element.73) | copy-start | bytes 786436
  221.2 3.5 %copy-start.21 = (bf16[512,256]{1,0:T(8,128)(2,1)S(1)}, bf16[512,256]{1,0:T(8,128)(2,1)}, u32[]{:S(2)}) copy-start(bf16[512,256]{1,0:T(8,128)(2,1)} %get-tuple-element.74) | copy-start | bytes 786436
  221.2 3.5 %copy-start.22 = (bf16[512,256]{1,0:T(8,128)(2,1)S(1)}, bf16[512,256]{1,0:T(8,128)(2,1)}, u32[]{:S(2)}) copy-start(bf16[512,256]{1,0:T(8,128)(2,1)} %get-tuple-element.75) | copy-start | bytes 786436
  221.2 3.5 %copy-start.23 = (bf16[512,256]{1,0:T(8,128)(2,1)S(1)}, bf16[512,256]{1,0:T(8,128)(2,1)}, u32[]{:S(2)}) copy-start(bf16[512,256]{1,0:T(8,128)(2,1)} %get-tuple-element.76) | copy-start | bytes 786436
  221.2 7.1 %slice-start = ((s8[10485760]{0:T(1024)(128)(4,1)}), s8[4194304]{0:T(1024)(128)(4,1)S(1)}, s32[]{:S(2)}) async-start(s8[10485760]{0:T(1024)(128)(4,1)} %bitcast.112), calls=%async_computation.2 | async-start | bytes 8388608
  221.2 7.1 %slice-start.1 = ((s8[10485760]{0:T(1024)(128)(4,1)}), s8[4194304]{0:T(1024)(128)(4,1)S(1)}, s32[]{:S(2)}) async-start(s8[10485760]{0:T(1024)(128)(4,1)} %bitcast.112), calls=%async_computation.3 | async-start | bytes 8388608
  224.7 3.6 %copy-start.2 = (bf16[512,256]{1,0:T(8,128)(2,1)S(1)}, bf16[512,256]{1,0:T(8,128)(2,1)}, u32[]{:S(2)}) copy-start(bf16[512,256]{1,0:T(8,128)(2,1)} %get-tuple-element.31) | copy-start | bytes 786436
  224.7 3.6 %copy-start.3 = (bf16[512,256]{1,0:T(8,128)(2,1)S(1)}, bf16[512,256]{1,0:T(8,128)(2,1)}, u32[]{:S(2)}) copy-start(bf16[512,256]{1,0:T(8,128)(2,1)} %get-tuple-element.32) | copy-start | bytes 786436
  224.7 3.6 %copy-start.4 = (bf16[512,256]{1,0:T(8,128)(2,1)S(1)}, bf16[512,256]{1,0:T(8,128)(2,1)}, u32[]{:S(2)}) copy-start(bf16[512,256]{1,0:T(8,128)(2,1)} %get-tuple-element.33) | copy-start | bytes 786436
  224.7 3.6 %copy-start.5 = (bf16[512,256]{1,0:T(8,128)(2,1)S(1)}, bf16[512,256]{1,0:T(8,128)(2,1)}, u32[]{:S(2)}) copy-start(bf16[512,256]{1,0:T(8,128)(2,1)} %get-tuple-element.34) | copy-start | bytes 786436
  224.8 3.6 %copy-start.6 = (bf16[512,256]{1,0:T(8,128)(2,1)S(1)}, bf16[512,256]{1,0:T(8,128)(2,1)}, u32[]{:S(2)}) copy-start(bf16[512,256]{1,0:T(8,128)(2,1)} %get-tuple-element.35) | copy-start | bytes 786436
  224.8 3.6 %copy-start.7 = (bf16[512,256]{1,0:T(8,128)(2,1)S(1)}, bf16[512,256]{1,0:T(8,128)(2,1)}, u32[]{:S(2)}) copy-start(bf16[512,256]{1,0:T(8,128)(2,1)} %get-tuple-element.36) | copy-start | bytes 786436
  224.8 3.6 %slice-start.2 = ((s8[10485760]{0:T(1024)(128)(4,1)}), s8[2097152]{0:T(1024)(128)(4,1)S(1)}, s32[]{:S(2)}) async-start(s8[10485760]{0:T(1024)(128)(4,1)} %bitcast.112), calls=%async_computation.4 | async-start | bytes 4194304
  241.8 3.4 %copy-start.26 = (f32[1024]{0:T(1024)S(1)}, f32[1024]{0:T(1024)}, u32[]{:S(2)}) copy-start(f32[1024]{0:T(1024)} %param.17) | copy-start | bytes 12292
  245.9 0.7 copy-start.27
  250.9 1.8 copy-start.28
  252.7 4.0 %copy-start.1 = (bf16[512,2048]{1,0:T(8,128)(2,1)S(1)}, bf16[512,2048]{1,0:T(8,128)(2,1)}, u32[]{:S(2)}) copy-start(bf16[512,2048]{1,0:T(8,128)(2,1)} %param.10) | copy-start | bytes 6291460
Sparse Core Ops, SparseCore 0:
  9.5 80.7 all-gather.2

commit v5 on v3

--- a/solution.py
+++ b/solution.py
@@ -158,11 +158,26 @@
             part = project(normed, k, tp_index, core_index)
             projected = part if projected is None else projected + part
         projected = lax.optimization_barrier(projected)
+        far_quarter = (tp_index - 2) % tp_count
+        far_rows = jnp.concatenate(
+            [
+                lax.dynamic_index_in_dim(own_rows, far_quarter, axis=0, keepdims=False),
+                lax.dynamic_index_in_dim(other_rows, far_quarter, axis=0, keepdims=False),
+            ],
+            axis=0,
+        )
         far_piece, far_scale, far_gain, far_tp, far_core = lax.optimization_barrier(
             (pieces[2], scale, norm_gain, tp_index, core_index)
         )
         normed = normalize(far_piece, 2, far_scale, far_gain, far_tp)
-        projected = projected + project(normed, 2, far_tp, far_core)
+        first = core_block(normed, 0)
+        second = core_block(normed, 1)
+        both = jnp.where(
+            far_core == 0,
+            jnp.concatenate([first, second], axis=1),
+            jnp.concatenate([second, first], axis=1),
+        )
+        projected = projected + jnp.dot(both, far_rows, preferred_element_type=jnp.float32)
         queries = projected[:, :q_cols]
         key_proj = projected[:, q_cols : q_cols + k_cols]
         value_proj = projected[:, q_cols + k_cols :]

time: 270 us -> 256 us (0.948)
  the two profiles are of different devices: /device:TPU:0 before, /device:TPU:49 now
where the time goes in v5:
time: 256 us; the launch traced here: 251 us
  waiting for transfers between devices  159 us (62%)
  matrix products  30.4 us (12%)
  other arithmetic  17.8 us (7%)
  starting transfers between devices  17.2 us (7%)
  between operations  14.2 us (6%)
  local copies, waits for them, and re-layouts  12.7 us (5%)
    all_gather x1, waiting for transfers between devices, body(): own_weights = lax.all_gather(weights, CHIPS, axis=0, tiled=False)  99.3 us
    ppermute x3, waiting for transfers between devices, body(): lax.ppermute(own_sq, TP, [(t, (t + k) % tp_count) for t in range(tp_count)])  43.8 us
    dot_general x6, matrix products, project(): part = jnp.dot(cols, rows, preferred_element_type=jnp.float32)  17.3 us
    ppermute x1, waiting for transfers between devices, body(): far_b = lax.ppermute(from_right[:, half:], TP, to_left)  12 us
    all_to_all x1, starting transfers between devices, body(): lax.all_to_all(payload, SEQ, split_axis=0, concat_axis=0, tiled=True)  8.27 us
    convert_element_type x2, other arithmetic, normalize(): return (piece.astype(jnp.float32) * scale * gain).astype(jnp.bfloat16)  5.23 us
  transfers between devices with their start and end apart: 10, of which 6 were waited for; matrix products, arithmetic and copies ran while one was open for 13% of the time, Pallas kernels for 0%

profile of v5, /device:TPU:49, one launch (start us, length us, event | category | flops | bytes accessed | tf_op | source)
XLA Modules:
  0.0 251.0 jit_solution(1555912897718623257)
XLA Ops:
  6.5 2.1 pad_maximum_fusion.7
  8.7 0.7 fusion.83
  9.4 1.2 reduce-window.15
  10.6 0.2 slice_reduce_fusion
  10.8 0.1 fusion.75
  11.0 0.2 select_reduce_fusion
  11.2 0.1 reshape.275
  11.4 0.1 concatenate.65
  11.5 1.8 convolution_convert_fusion
  13.3 2.0 broadcast_select_fusion
  15.3 8.3 %all-to-all-start = ((bf16[32,24,2048]{2,1,0:T(8,128)(2,1)}), bf16[32,24,2048]{2,1,0:T(8,128)(2,1)S(1)}, u32[]{:S(2)}, u32[]{:S(2)}) async-start(bf16[32,24,2048]{2,1,0:T(8,128)(2,1)} %broadcast_select_fusion), calls=%async_computation | async-start | bytes 6291456 | tf_op jit(solution)/shard_map/all_to_all | solution.py:89
  23.6 99.3 %all-gather.3.cloned.1.call-done = bf16[4096,1280]{1,0:T(8,128)(2,1)} async-done(((bf16[256,1280]{1,0:T(8,128)(2,1)}), bf16[4096,1280]{1,0:T(8,128)(2,1)}) %all-gather.3.cloned.1.call-update) | async-done | bytes 10485776 | tf_op jit(solution)/shard_map/all_gather | solution.py:59
  122.9 0.8 collective-permute-start.3
  123.7 0.1 fusion.79
  123.8 0.1 eq.112
  123.9 3.2 %fusion.6 = (f32[512]{0:T(512)S(1)}, bf16[512,2048]{1,0:T(8,128)(2,1)}) fusion(bf16[768,2048]{1,0:T(8,128)(2,1)S(1)} %bitcast.103, s32[768]{0:T(1024)S(1)} %eq.112), kind=kOutput, calls=%fused_computation.11 | convolution fusion | flops 1615199744 | bytes 5248000 | tf_op jit(solution)/shard_map/dot_general | solution.py:97
  127.1 2.4 collective-permute-start.5
  129.5 0.1 slice_compare_fusion.1
  129.6 0.1 add_select_fusion.4
  129.7 0.3 reduce-window.19
  130.0 0.1 slice.199
  130.1 0.1 slice_reduce_fusion.1
  130.2 0.1 fusion.84
  130.3 0.2 fusion.48
  130.5 1.0 multiply_cosine_fusion
  131.5 2.7 %collective-permute-start.2 = (f32[512]{0:T(512)S(1)}, f32[512]{0:T(512)S(1)}, u32[]{:S(2)}, u32[]{:S(2)}) collective-permute-start(f32[512]{0:T(512)S(1)} %get-tuple-element.73), channel_id=1, source_target_pairs={{0,3},{1,0},{2,1},{3,2},{4,7},{5,4},{6,5},{7,6},{8,11},{9,8},{10,9... | collective-permute-start | bytes 6152 | tf_op jit(solution)/shard_map/ppermute | solution.py:108
  134.3 40.5 %collective-permute-done.2 = f32[512]{0:T(512)S(1)} collective-permute-done((f32[512]{0:T(512)S(1)}, f32[512]{0:T(512)S(1)}, u32[]{:S(2)}, u32[]{:S(2)}) %collective-permute-start.2) | collective-permute-done | bytes 2080 | tf_op jit(solution)/shard_map/ppermute | solution.py:108
  174.7 1.1 collective-permute-start
  175.9 0.8 collective-permute-done.1
  176.7 2.5 %collective-permute-done = f32[512]{0:T(512)S(1)} collective-permute-done((f32[512]{0:T(512)S(1)}, f32[512]{0:T(512)S(1)}, u32[]{:S(2)}, u32[]{:S(2)}) %collective-permute-start) | collective-permute-done | bytes 2080 | tf_op jit(solution)/shard_map/ppermute | solution.py:108
  179.2 0.1 slice.235
  179.3 1.5 collective-permute-start.7
  180.9 1.3 slice.234
  182.2 0.3 collective-permute-start.6
  182.4 4.7 %fusion.8 = (bf16[512,2048]{1,0:T(8,128)(2,1)S(1)}, bf16[512,2048]{1,0:T(8,128)(2,1)S(1)}, bf16[512,2048]{1,0:T(8,128)(2,1)S(1)}) fusion(bf16[512,2048]{1,0:T(8,128)(2,1)} %get-tuple-element.74, f32[2048]{0:T(1024)S(1)} %get-tuple-element.63, f32[512]{0:T(512)S(1)} %add_rsqrt_fusion, f32[2048]{0:T(1024)S(1)} %get-tuple-element.64, ...), kind=kLoop, calls=%fused_computation.13 | loop fusion | flops 12582912 | bytes 12609536 | tf_op jit(solution)/shard_map/convert_element_type | solution.py:140
  187.1 1.3 fusion.105
  188.5 1.9 fusion.103
  190.3 12.0 %collective-permute-done.7 = bf16[512,1024]{1,0:T(8,128)(2,1)S(1)} collective-permute-done((bf16[512,1024]{1,0:T(8,128)(2,1)S(1)}, bf16[512,1024]{1,0:T(8,128)(2,1)S(1)}, u32[]{:S(2)}, u32[]{:S(2)}) %collective-permute-start.7) | collective-permute-done | bytes 1048608 | tf_op jit(solution)/shard_map/ppermute | solution.py:122
  202.4 3.7 %collective-permute-done.6 = bf16[512,1024]{1,0:T(8,128)(2,1)S(1)} collective-permute-done((bf16[512,1024]{1,0:T(8,128)(2,1)S(1)}, bf16[512,1024]{1,0:T(8,128)(2,1)S(1)}, u32[]{:S(2)}, u32[]{:S(2)}) %collective-permute-start.6) | collective-permute-done | bytes 1048608 | tf_op jit(solution)/shard_map/ppermute | solution.py:121
  206.1 0.2 pad_maximum_fusion
  206.3 0.5 multiply_convert_fusion
  206.8 0.1 slice_dynamic-update-slice_fusion.6
  206.9 0.1 slice_dynamic-update-slice_fusion.4
  207.4 0.1 slice_dynamic-update-slice_fusion.8
  207.5 2.1 dynamic-slice_bitcast_fusion.1
  209.8 4.1 %fusion.18 = f32[512,1280]{1,0:T(8,128)S(1)} fusion(bf16[4,1024,1280]{2,1,0:T(8,128)(2,1)} %bitcast.108, s32[]{:T(128)S(6)} %select_n.152, pred[]{:T(512)S(6)} %eq.100, bf16[512,256]{1,0:T(8,128)(2,1)S(1)} %copy-done.9, bf16[512,256]{1,0:T(8,128)(2,1)S(1)} %copy-done.10, bf16[512,256]{1,0:T(8,128)(2,1)S(1)} %copy-done.11, ...), kind=kOutput, calls=%fused_computation.30 | convolution fusion | flops 1351090176 | bytes 7340037 | tf_op jit(solution)/shard_map/dot_general | solution.py:151
  213.9 0.1 copy-done.22
  214.0 0.1 copy-done.23
  214.1 1.6 fusion.21
  215.7 1.6 fusion.24
  217.3 1.9 dynamic-slice_bitcast_fusion
  219.2 3.3 %convolution_add_fusion = f32[512,1280]{1,0:T(8,128)S(1)} fusion(f32[512,1280]{1,0:T(8,128)S(1)} %fusion.18, bf16[4,1024,1280]{2,1,0:T(8,128)(2,1)} %bitcast.9, s32[]{:T(128)S(6)} %select_n.152, pred[]{:T(512)S(6)} %eq.100, bf16[512,256]{1,0:T(8,128)(2,1)S(1)} %copy-done.9, bf16[512,256]{1,0:T(8,128)(2,1)S(1)} %copy-done.10, ...), kind=kOutput, calls=%fused_computation.21 | convolution fusion | flops 1351745536 | bytes 9961477 | tf_op jit(solution)/shard_map/dot_general | solution.py:151
  222.6 3.3 %convolution_add_fusion.1 = f32[512,1280]{1,0:T(8,128)S(1)} fusion(f32[512,1280]{1,0:T(8,128)S(1)} %fusion.21, bf16[4,1024,1280]{2,1,0:T(8,128)(2,1)} %bitcast.9, s32[]{:T(128)S(6)} %select_n.147, pred[]{:T(512)S(6)} %eq.100, bf16[512,256]{1,0:T(8,128)(2,1)S(1)} %copy-done.22, bf16[512,256]{1,0:T(8,128)(2,1)S(1)} %copy-done.21, ...), kind=kOutput, calls=%fused_computation.22 | convolution fusion | flops 1351745536 | bytes 9961477 | tf_op jit(solution)/shard_map/dot_general | solution.py:151
  225.9 3.5 %fusion.16 = f32[512,1280]{1,0:T(8,128)S(1)} fusion(f32[512,1280]{1,0:T(8,128)S(1)} %convolution_add_fusion, f32[512,1280]{1,0:T(8,128)S(1)} %convolution_add_fusion.1, f32[512,1280]{1,0:T(8,128)S(1)} %fusion.24, bf16[4,1024,1280]{2,1,0:T(8,128)(2,1)} %bitcast.9, s32[]{:T(128)S(6)} %select_n.142, pred[]{:T(512)S(6)} %eq.100, ...), kind=kOutput, calls=%fused_computation.26 | convolution fusion | flops 1353056256 | bytes 15204357 | tf_op jit(solution)/shard_map/dot_general | solution.py:151
  229.4 3.2 %fusion.13 = f32[512,1280]{1,0:T(8,128)S(1)} fusion(f32[512,1280]{1,0:T(8,128)S(1)} %fusion.16, bf16[1024,1280]{1,0:T(8,128)(2,1)S(1)} %dynamic-slice_bitcast_fusion, bf16[1024,1280]{1,0:T(8,128)(2,1)S(1)} %dynamic-slice_bitcast_fusion.1, bf16[512,2048]{1,0:T(8,128)(2,1)S(1)} %get-tuple-element.22, bf16[512,2048]{1,0:T(8,128)(2,1)S(1)} %get-tuple-element.21, ...), kind=kOutput, calls=%fused_computation.25 | convolution fusion | flops 2696544256 | bytes 14680065 | tf_op jit(solution)/shard_map/dot_general | solution.py:180
  232.6 0.3 fusion.32
  232.9 0.5 copy.52
  233.4 0.7 fusion.102
  234.2 1.2 fusion.73
  235.4 0.8 subtract_convert_fusion
  236.2 2.2 fusion.1
  238.4 1.7 fusion
  240.2 2.7 %fusion.35 = bf16[128,8,512]{2,0,1:T(8,128)(2,1)S(1)} fusion(f32[8,512]{1,0:T(8,128)S(1)} %fusion, f32[8,512]{1,0:T(8,128)S(1)} %get-tuple-element.75, f32[512,512,8]{1,0,2:T(8,128)S(1)} %get-tuple-element.76, pred[512,512]{0,1:T(8,128)(4,1)S(1)} %fusion.48, f32[512,1280]{1,0:T(8,128)S(1)} %fusion.13, f32[128]{0:T(128)S(1)} %copy-done.28), kind=kOutput, calls=%fused_computation.56 | convolution fusion | flops 548012032 | bytes 9994752 | tf_op jit(solution)/shard_map/kgqp,pkd->qkgd/dot_general | solution.py:208
  242.9 1.3 copy.44
  (93 shorter events, 0.7 us)
Async XLA Ops:
  6.5 5.0 %copy-start = (bf16[512,2048]{1,0:T(8,128)(2,1)S(1)}, bf16[512,2048]{1,0:T(8,128)(2,1)}, u32[]{:S(2)}) copy-start(bf16[512,2048]{1,0:T(8,128)(2,1)} %param.10) | copy-start | bytes 6291460
  6.5 116.3 %all-gather.3.cloned.1.call-start = ((), (), s32[]{:S(2)}) async-start(), calls=%async_computation.1 | async-start | bytes 11141120 | tf_op jit(solution)/shard_map/all_gather | solution.py:59
  15.3 108.4 %all-to-all-start = ((bf16[32,24,2048]{2,1,0:T(8,128)(2,1)}), bf16[32,24,2048]{2,1,0:T(8,128)(2,1)S(1)}, u32[]{:S(2)}, u32[]{:S(2)}) async-start(bf16[32,24,2048]{2,1,0:T(8,128)(2,1)} %broadcast_select_fusion), calls=%async_computation | async-start | bytes 6291456 | tf_op jit(solution)/shard_map/all_to_all | solution.py:89
  122.9 94.5 %collective-permute-start.3 = (bf16[16,256,1280]{2,1,0:T(8,128)(2,1)}, bf16[16,256,1280]{2,1,0:T(8,128)(2,1)}, u32[]{:S(2)}, u32[]{:S(2)}) collective-permute-start(bf16[16,256,1280]{2,1,0:T(8,128)(2,1)} %bitcast.106), channel_id=1, source_target_pairs={{0,4},{4,0},{1,5},{5,1},{2,6},{6,2},{3,7},{7,3},{8,12},{12,8},{9,1... | collective-permute-start | bytes 31457288 | tf_op jit(solution)/shard_map/ppermute | solution.py:60
  123.9 5.6 %copy-start.24 = (s32[512]{0:T(512)S(1)}, s32[512]{0:T(512)}, u32[]{:S(2)}) copy-start(s32[512]{0:T(512)} %param.12) | copy-start | bytes 6148
  123.9 51.9 %copy-start.25 = (f32[8192]{0:T(1024)S(1)}, f32[8192]{0:T(1024)}, u32[]{:S(2)}) copy-start(f32[8192]{0:T(1024)} %param.13) | copy-start | bytes 98308
  127.1 52.1 %collective-permute-start.5 = (bf16[512,2048]{1,0:T(8,128)(2,1)}, bf16[512,2048]{1,0:T(8,128)(2,1)S(1)}, u32[]{:S(2)}, u32[]{:S(2)}) collective-permute-start(bf16[512,2048]{1,0:T(8,128)(2,1)} %get-tuple-element.74), channel_id=1, source_target_pairs={{0,3},{1,0},{2,1},{3,2},{4,7},{5,4},{6,5},{7,6},{8,11},{9,8},{10,9... | collective-permute-start | bytes 6291464 | tf_op jit(solution)/shard_map/ppermute | solution.py:120
  129.5 51.3 %collective-permute-start.4 = (bf16[512,2048]{1,0:T(8,128)(2,1)}, bf16[512,2048]{1,0:T(8,128)(2,1)}, u32[]{:S(2)}, u32[]{:S(2)}) collective-permute-start(bf16[512,2048]{1,0:T(8,128)(2,1)} %get-tuple-element.74), channel_id=1, source_target_pairs={{0,1},{1,2},{2,3},{3,0},{4,5},{5,6},{6,7},{7,4},{8,9},{9,10},{10,1... | collective-permute-start | bytes 6291464 | tf_op jit(solution)/shard_map/ppermute | solution.py:119
  131.5 43.2 %collective-permute-start.2 = (f32[512]{0:T(512)S(1)}, f32[512]{0:T(512)S(1)}, u32[]{:S(2)}, u32[]{:S(2)}) collective-permute-start(f32[512]{0:T(512)S(1)} %get-tuple-element.73), channel_id=1, source_target_pairs={{0,3},{1,0},{2,1},{3,2},{4,7},{5,4},{6,5},{7,6},{8,11},{9,8},{10,9... | collective-permute-start | bytes 6152 | tf_op jit(solution)/shard_map/ppermute | solution.py:108
  134.3 42.4 %collective-permute-start.1 = (f32[512]{0:T(512)S(1)}, f32[512]{0:T(512)S(1)}, u32[]{:S(2)}, u32[]{:S(2)}) collective-permute-start(f32[512]{0:T(512)S(1)} %get-tuple-element.73), channel_id=1, source_target_pairs={{0,2},{1,3},{2,0},{3,1},{4,6},{5,7},{6,4},{7,5},{8,10},{9,11},{10,... | collective-permute-start | bytes 6152 | tf_op jit(solution)/shard_map/ppermute | solution.py:108
  174.7 4.5 %collective-permute-start = (f32[512]{0:T(512)S(1)}, f32[512]{0:T(512)S(1)}, u32[]{:S(2)}, u32[]{:S(2)}) collective-permute-start(f32[512]{0:T(512)S(1)} %get-tuple-element.73), channel_id=1, source_target_pairs={{0,1},{1,2},{2,3},{3,0},{4,5},{5,6},{6,7},{7,4},{8,9},{9,10},{10,1... | collective-permute-start | bytes 6152 | tf_op jit(solution)/shard_map/ppermute | solution.py:108
  179.3 23.1 %collective-permute-start.7 = (bf16[512,1024]{1,0:T(8,128)(2,1)S(1)}, bf16[512,1024]{1,0:T(8,128)(2,1)S(1)}, u32[]{:S(2)}, u32[]{:S(2)}) collective-permute-start(bf16[512,1024]{1,0:T(8,128)(2,1)S(1)} %slice.235), channel_id=1, source_target_pairs={{0,3},{1,0},{2,1},{3,2},{4,7},{5,4},{6,5},{7,6},{8,11},{9,8},{10,9... | collective-permute-start | bytes 3145736 | tf_op jit(solution)/shard_map/ppermute | solution.py:122
  182.2 23.9 %collective-permute-start.6 = (bf16[512,1024]{1,0:T(8,128)(2,1)S(1)}, bf16[512,1024]{1,0:T(8,128)(2,1)S(1)}, u32[]{:S(2)}, u32[]{:S(2)}) collective-permute-start(bf16[512,1024]{1,0:T(8,128)(2,1)S(1)} %slice.234), channel_id=1, source_target_pairs={{0,1},{1,2},{2,3},{3,0},{4,5},{5,6},{6,7},{7,4},{8,9},{9,10},{10,1... | collective-permute-start | bytes 3145736 | tf_op jit(solution)/shard_map/ppermute | solution.py:121
  207.2 2.4 copy-start.12
  207.2 2.4 copy-start.13
  207.2 2.4 copy-start.14
  207.2 2.4 copy-start.15
  207.3 6.5 %slice-start = ((s8[10485760]{0:T(1024)(128)(4,1)}), s8[2097152]{0:T(1024)(128)(4,1)S(1)}, s32[]{:S(2)}) async-start(s8[10485760]{0:T(1024)(128)(4,1)} %bitcast.109), calls=%async_computation.2 | async-start | bytes 4194304
  207.5 2.2 copy-start.8
  207.5 2.2 copy-start.9
  207.5 2.2 copy-start.10
  207.5 2.2 copy-start.11
  207.5 6.3 %slice-start.1 = ((s8[10485760]{0:T(1024)(128)(4,1)}), s8[4194304]{0:T(1024)(128)(4,1)S(1)}, s32[]{:S(2)}) async-start(s8[10485760]{0:T(1024)(128)(4,1)} %bitcast.109), calls=%async_computation.3 | async-start | bytes 8388608
  209.7 4.2 %slice-start.2 = ((s8[10485760]{0:T(1024)(128)(4,1)}), s8[4194304]{0:T(1024)(128)(4,1)S(1)}, s32[]{:S(2)}) async-start(s8[10485760]{0:T(1024)(128)(4,1)} %bitcast.109), calls=%async_computation.4 | async-start | bytes 8388608
  209.7 4.2 %copy-start.16 = (bf16[512,256]{1,0:T(8,128)(2,1)S(1)}, bf16[512,256]{1,0:T(8,128)(2,1)}, u32[]{:S(2)}) copy-start(bf16[512,256]{1,0:T(8,128)(2,1)} %get-tuple-element.77) | copy-start | bytes 786436
  209.7 4.2 %copy-start.17 = (bf16[512,256]{1,0:T(8,128)(2,1)S(1)}, bf16[512,256]{1,0:T(8,128)(2,1)}, u32[]{:S(2)}) copy-start(bf16[512,256]{1,0:T(8,128)(2,1)} %get-tuple-element.78) | copy-start | bytes 786436
  209.7 4.2 %copy-start.18 = (bf16[512,256]{1,0:T(8,128)(2,1)S(1)}, bf16[512,256]{1,0:T(8,128)(2,1)}, u32[]{:S(2)}) copy-start(bf16[512,256]{1,0:T(8,128)(2,1)} %get-tuple-element.79) | copy-start | bytes 786436
  209.7 4.2 %copy-start.19 = (bf16[512,256]{1,0:T(8,128)(2,1)S(1)}, bf16[512,256]{1,0:T(8,128)(2,1)}, u32[]{:S(2)}) copy-start(bf16[512,256]{1,0:T(8,128)(2,1)} %get-tuple-element.80) | copy-start | bytes 786436
  209.7 4.2 %copy-start.20 = (bf16[512,256]{1,0:T(8,128)(2,1)S(1)}, bf16[512,256]{1,0:T(8,128)(2,1)}, u32[]{:S(2)}) copy-start(bf16[512,256]{1,0:T(8,128)(2,1)} %get-tuple-element.81) | copy-start | bytes 786436
  209.7 4.2 %copy-start.21 = (bf16[512,256]{1,0:T(8,128)(2,1)S(1)}, bf16[512,256]{1,0:T(8,128)(2,1)}, u32[]{:S(2)}) copy-start(bf16[512,256]{1,0:T(8,128)(2,1)} %get-tuple-element.82) | copy-start | bytes 786436
  209.7 4.3 %copy-start.22 = (bf16[512,256]{1,0:T(8,128)(2,1)S(1)}, bf16[512,256]{1,0:T(8,128)(2,1)}, u32[]{:S(2)}) copy-start(bf16[512,256]{1,0:T(8,128)(2,1)} %get-tuple-element.83) | copy-start | bytes 786436
  209.7 4.3 %copy-start.23 = (bf16[512,256]{1,0:T(8,128)(2,1)S(1)}, bf16[512,256]{1,0:T(8,128)(2,1)}, u32[]{:S(2)}) copy-start(bf16[512,256]{1,0:T(8,128)(2,1)} %get-tuple-element.84) | copy-start | bytes 786436
  214.1 1.6 copy-start.2
  214.1 1.6 copy-start.3
  214.1 1.6 copy-start.4
  214.1 1.6 copy-start.5
  214.1 1.6 copy-start.6
  214.1 1.6 copy-start.7
  229.4 3.3 %copy-start.26 = (f32[1024]{0:T(1024)S(1)}, f32[1024]{0:T(1024)}, u32[]{:S(2)}) copy-start(f32[1024]{0:T(1024)} %param.17) | copy-start | bytes 12292
  233.4 0.7 copy-start.27
  238.4 1.8 copy-start.28
  240.2 4.0 %copy-start.1 = (bf16[512,2048]{1,0:T(8,128)(2,1)S(1)}, bf16[512,2048]{1,0:T(8,128)(2,1)}, u32[]{:S(2)}) copy-start(bf16[512,2048]{1,0:T(8,128)(2,1)} %param.10) | copy-start | bytes 6291460
Sparse Core Ops, SparseCore 0:
  9.5 113.2 all-gather.2

commit v6 on v3

--- a/solution.py
+++ b/solution.py
@@ -115,12 +115,16 @@
 
         to_right = [(t, (t + 1) % tp_count) for t in range(tp_count)]
         to_left = [(t, (t - 1) % tp_count) for t in range(tp_count)]
-        half = width // 2
-        from_left = lax.ppermute(learner_part, TP, to_right)
-        from_right = lax.ppermute(learner_part, TP, to_left)
-        far_a = lax.ppermute(from_left[:, :half], TP, to_right)
-        far_b = lax.ppermute(from_right[:, half:], TP, to_left)
-        far = jnp.concatenate([far_a, far_b], axis=1)
+        half_rows = row_count // 2
+        left_top = lax.ppermute(learner_part[:half_rows], TP, to_right)
+        left_bottom = lax.ppermute(learner_part[half_rows:], TP, to_left)
+        right_top = lax.ppermute(learner_part[:half_rows], TP, to_left)
+        right_bottom = lax.ppermute(learner_part[half_rows:], TP, to_right)
+        from_left = jnp.concatenate([left_top, right_bottom], axis=0)
+        from_right = jnp.concatenate([right_top, left_bottom], axis=0)
+        far_a = lax.ppermute(left_top, TP, to_right)
+        far_b = lax.ppermute(left_bottom, TP, to_left)
+        far = jnp.concatenate([far_a, far_b], axis=0)
         pieces = [learner_part, from_left, far, from_right]
 
         block = width // (4 * core_count)

time: 270 us -> 271 us (level)
  the two profiles are of different devices: /device:TPU:0 before, /device:TPU:49 now
where the time goes in v6:
time: 271 us; the launch traced here: 266 us
  waiting for transfers between devices  170 us (63%)
  matrix products  33.9 us (13%)
  starting transfers between devices  19.5 us (7%)
  other arithmetic  17.8 us (7%)
  between operations  14.2 us (5%)
  local copies, waits for them, and re-layouts  10.8 us (4%)
    all_gather x1, waiting for transfers between devices, body(): own_weights = lax.all_gather(weights, CHIPS, axis=0, tiled=False)  78.8 us
    all_to_all x1, waiting for transfers between devices, body(): lax.all_to_all(payload, SEQ, split_axis=0, concat_axis=0, tiled=True)  35.9 us
    dot_general x8, matrix products, project(): part = jnp.dot(cols, rows, preferred_element_type=jnp.float32)  23.5 us
    ppermute x1, waiting for transfers between devices, body(): left_top = lax.ppermute(learner_part[:half_rows], TP, to_right)  20.2 us
    ppermute x1, waiting for transfers between devices, body(): left_bottom = lax.ppermute(learner_part[half_rows:], TP, to_left)  18.1 us
    ppermute x1, waiting for transfers between devices, body(): far_b = lax.ppermute(left_bottom, TP, to_left)  14.8 us
    all_to_all x1, starting transfers between devices, body(): lax.all_to_all(payload, SEQ, split_axis=0, concat_axis=0, tiled=True)  7.07 us
  transfers between devices with their start and end apart: 12, of which 6 were waited for; matrix products, arithmetic and copies ran while one was open for 13% of the time, Pallas kernels for 0%

profile of v6, /device:TPU:49, one launch (start us, length us, event | category | flops | bytes accessed | tf_op | source)
XLA Modules:
  0.0 266.2 jit_solution(10901829865181630873)
XLA Ops:
  6.5 2.1 pad_maximum_fusion.9
  8.7 0.7 fusion.84
  9.4 1.2 reduce-window.15
  10.6 0.2 slice_reduce_fusion
  10.8 0.1 fusion.76
  11.0 0.2 select_reduce_fusion
  11.2 0.1 reshape.275
  11.4 0.1 concatenate.64
  11.5 78.8 %all-gather.3.cloned.1.call-done = bf16[4096,1280]{1,0:T(8,128)(2,1)} async-done(((bf16[256,1280]{1,0:T(8,128)(2,1)}), bf16[4096,1280]{1,0:T(8,128)(2,1)}) %all-gather.3.cloned.1.call-update) | async-done | bytes 10485776 | tf_op jit(solution)/shard_map/all_gather | solution.py:59
  90.3 0.8 collective-permute-start.3
  91.1 1.8 convolution_convert_fusion
  92.9 2.1 broadcast_select_fusion
  95.0 7.1 %all-to-all-start = ((bf16[32,24,2048]{2,1,0:T(8,128)(2,1)}), bf16[32,24,2048]{2,1,0:T(8,128)(2,1)}, u32[]{:S(2)}, u32[]{:S(2)}) async-start(bf16[32,24,2048]{2,1,0:T(8,128)(2,1)} %broadcast_select_fusion), calls=%async_computation | async-start | bytes 6291456 | tf_op jit(solution)/shard_map/all_to_all | solution.py:89
  102.2 0.3 reduce-window.19
  102.6 0.1 slice_reduce_fusion.1
  102.8 35.9 %all-to-all-done = bf16[32,24,2048]{2,1,0:T(8,128)(2,1)} async-done(((bf16[32,24,2048]{2,1,0:T(8,128)(2,1)}), bf16[32,24,2048]{2,1,0:T(8,128)(2,1)}, u32[]{:S(2)}, u32[]{:S(2)}) %all-to-all-start) | async-done | bytes 3145760 | tf_op jit(solution)/shard_map/all_to_all | solution.py:89
  138.6 0.9 slice.209
  139.6 0.1 eq.113
  139.7 3.8 %fusion.2 = (f32[512]{0:T(512)S(1)}, bf16[512,2048]{1,0:T(8,128)(2,1)S(1)}) fusion(bf16[768,2048]{1,0:T(8,128)(2,1)} %bitcast.5, s32[768]{0:T(1024)S(1)} %eq.113), kind=kOutput, calls=%fused_computation.7 | convolution fusion | flops 1615199744 | bytes 5248000 | tf_op jit(solution)/shard_map/dot_general | solution.py:97
  143.5 2.5 collective-permute-start.2
  145.9 0.6 collective-permute-start.1
  146.5 0.6 collective-permute-start
  147.1 1.6 fusion.111
  148.7 1.5 collective-permute-start.5
  150.2 1.2 collective-permute-start.7
  151.4 0.3 collective-permute-start.4
  151.7 2.4 collective-permute-start.6
  154.2 0.2 fusion.47
  154.4 1.8 multiply_cosine_fusion
  156.2 18.1 %collective-permute-done.7 = bf16[256,2048]{1,0:T(8,128)(2,1)S(1)} collective-permute-done((bf16[256,2048]{1,0:T(8,128)(2,1)}, bf16[256,2048]{1,0:T(8,128)(2,1)S(1)}, u32[]{:S(2)}, u32[]{:S(2)}) %collective-permute-start.7) | collective-permute-done | bytes 1048608 | tf_op jit(solution)/shard_map/ppermute | solution.py:120
  174.3 2.3 collective-permute-start.9
  176.6 20.2 %collective-permute-done.4 = bf16[256,2048]{1,0:T(8,128)(2,1)} collective-permute-done((bf16[256,2048]{1,0:T(8,128)(2,1)}, bf16[256,2048]{1,0:T(8,128)(2,1)}, u32[]{:S(2)}, u32[]{:S(2)}) %collective-permute-start.4) | collective-permute-done | bytes 1048608 | tf_op jit(solution)/shard_map/ppermute | solution.py:119
  196.8 0.3 collective-permute-start.8
  197.0 3.9 %fusion.4 = (bf16[512,2048]{1,0:T(8,128)(2,1)S(1)}, bf16[512,2048]{1,0:T(8,128)(2,1)S(1)}, bf16[512,2048]{1,0:T(8,128)(2,1)S(1)}) fusion(bf16[512,2048]{1,0:T(8,128)(2,1)S(1)} %get-tuple-element.68, f32[2048]{0:T(1024)S(1)} %get-tuple-element.57, f32[512]{0:T(512)S(1)} %add_rsqrt_fusion, f32[2048]{0:T(1024)S(1)} %get-tuple-element.58, ...), kind=kLoop, calls=%fused_computation.9 | loop fusion | flops 18874368 | bytes 12609536 | tf_op jit(solution)/shard_map/convert_element_type | solution.py:144
  201.0 1.3 fusion.110
  202.3 2.0 fusion.108
  204.3 14.8 %collective-permute-done.9 = bf16[256,2048]{1,0:T(8,128)(2,1)S(1)} collective-permute-done((bf16[256,2048]{1,0:T(8,128)(2,1)S(1)}, bf16[256,2048]{1,0:T(8,128)(2,1)S(1)}, u32[]{:S(2)}, u32[]{:S(2)}) %collective-permute-start.9) | collective-permute-done | bytes 1048608 | tf_op jit(solution)/shard_map/ppermute | solution.py:126
  219.1 2.3 collective-permute-done.8
  221.4 0.1 pad_maximum_fusion
  221.6 0.5 multiply_convert_fusion
  222.2 0.1 fusion.107
  222.4 0.7 copy-done.12
  223.2 0.1 copy-done.14
  223.2 0.1 copy-done.15
  223.3 0.1 copy-done.16
  223.5 0.1 copy-done.18
  223.6 0.1 copy-done.19
  223.7 3.4 %fusion.15 = f32[512,1280]{1,0:T(8,128)S(1)} fusion(bf16[4,1024,1280]{2,1,0:T(8,128)(2,1)} %bitcast.109, s32[]{:T(128)S(6)} %select_n.152, pred[]{:T(512)S(6)} %eq.101, bf16[512,256]{1,0:T(8,128)(2,1)S(1)} %copy-done.13, bf16[512,256]{1,0:T(8,128)(2,1)S(1)} %copy-done.14, bf16[512,256]{1,0:T(8,128)(2,1)S(1)} %copy-done.15, ...), kind=kOutput, calls=%fused_computation.30 | convolution fusion | flops 1351090176 | bytes 7340037 | tf_op jit(solution)/shard_map/dot_general | solution.py:155
  227.3 3.5 %fusion.18 = f32[512,1280]{1,0:T(8,128)S(1)} fusion(bf16[4,1024,1280]{2,1,0:T(8,128)(2,1)} %bitcast.110, s32[]{:T(128)S(6)} %select_n.147, pred[]{:T(512)S(6)} %eq.101, bf16[512,256]{1,0:T(8,128)(2,1)S(1)} %copy-done.26, bf16[512,256]{1,0:T(8,128)(2,1)S(1)} %copy-done.25, bf16[512,256]{1,0:T(8,128)(2,1)S(1)} %copy-done.24, ...), kind=kOutput, calls=%fused_computation.33 | convolution fusion | flops 1351090176 | bytes 7340037 | tf_op jit(solution)/shard_map/dot_general | solution.py:155
  231.0 1.6 fusion.21
  232.6 1.5 fusion.12
  234.1 3.3 %convolution_add_fusion.1 = f32[512,1280]{1,0:T(8,128)S(1)} fusion(f32[512,1280]{1,0:T(8,128)S(1)} %fusion.15, bf16[4,1024,1280]{2,1,0:T(8,128)(2,1)} %bitcast.9, s32[]{:T(128)S(6)} %select_n.152, pred[]{:T(512)S(6)} %eq.101, bf16[512,256]{1,0:T(8,128)(2,1)S(1)} %copy-done.13, bf16[512,256]{1,0:T(8,128)(2,1)S(1)} %copy-done.14, ...), kind=kOutput, calls=%fused_computation.18 | convolution fusion | flops 1351745536 | bytes 9961477 | tf_op jit(solution)/shard_map/dot_general | solution.py:155
  237.4 3.3 %convolution_add_fusion.2 = f32[512,1280]{1,0:T(8,128)S(1)} fusion(f32[512,1280]{1,0:T(8,128)S(1)} %fusion.18, bf16[4,1024,1280]{2,1,0:T(8,128)(2,1)} %bitcast.9, s32[]{:T(128)S(6)} %select_n.147, pred[]{:T(512)S(6)} %eq.101, bf16[512,256]{1,0:T(8,128)(2,1)S(1)} %copy-done.26, bf16[512,256]{1,0:T(8,128)(2,1)S(1)} %copy-done.25, ...), kind=kOutput, calls=%fused_computation.19 | convolution fusion | flops 1351745536 | bytes 9961477 | tf_op jit(solution)/shard_map/dot_general | solution.py:155
  240.7 3.5 %fusion.10 = f32[512,1280]{1,0:T(8,128)S(1)} fusion(f32[512,1280]{1,0:T(8,128)S(1)} %convolution_add_fusion.1, f32[512,1280]{1,0:T(8,128)S(1)} %convolution_add_fusion.2, f32[512,1280]{1,0:T(8,128)S(1)} %fusion.21, bf16[4,1024,1280]{2,1,0:T(8,128)(2,1)} %bitcast.9, s32[]{:T(128)S(6)} %select_n.142, pred[]{:T(512)S(6)} %eq.101, ...), kind=kOutput, calls=%fused_computation.23 | convolution fusion | flops 1353056256 | bytes 15204357 | tf_op jit(solution)/shard_map/dot_general | solution.py:155
  244.2 3.4 %fusion.9 = f32[512,1280]{1,0:T(8,128)S(1)} fusion(f32[512,1280]{1,0:T(8,128)S(1)} %fusion.10, f32[512,1280]{1,0:T(8,128)S(1)} %fusion.12, bf16[4,1024,1280]{2,1,0:T(8,128)(2,1)} %bitcast.9, s32[]{:T(128)S(6)} %select_n.158, pred[]{:T(512)S(6)} %eq.117, bf16[512,256]{1,0:T(8,128)(2,1)S(1)} %get-tuple-element.22, ...), kind=kOutput, calls=%fused_computation.22 | convolution fusion | flops 1352400896 | bytes 12582917 | tf_op jit(solution)/shard_map/dot_general | solution.py:155
  247.6 0.3 fusion.31
  247.9 0.7 copy.52
  248.6 0.7 fusion.106
  249.3 1.2 fusion.74
  250.6 0.8 subtract_convert_fusion
  251.4 2.2 fusion.1
  253.6 1.7 fusion
  255.3 2.7 %fusion.32 = bf16[128,8,512]{2,0,1:T(8,128)(2,1)S(1)} fusion(f32[8,512]{1,0:T(8,128)S(1)} %fusion, f32[8,512]{1,0:T(8,128)S(1)} %get-tuple-element.69, f32[512,512,8]{1,0,2:T(8,128)S(1)} %get-tuple-element.70, pred[512,512]{0,1:T(8,128)(4,1)S(1)} %fusion.47, f32[512,1280]{1,0:T(8,128)S(1)} %fusion.9, f32[128]{0:T(128)S(1)} %copy-done.32), kind=kOutput, calls=%fused_computation.54 | convolution fusion | flops 548012032 | bytes 9994752 | tf_op jit(solution)/shard_map/kgqp,pkd->qkgd/dot_general | solution.py:197
  258.0 1.3 copy.44
  (96 shorter events, 0.9 us)
Async XLA Ops:
  6.5 84.6 %copy-start = (bf16[512,2048]{1,0:T(8,128)(2,1)S(1)}, bf16[512,2048]{1,0:T(8,128)(2,1)}, u32[]{:S(2)}) copy-start(bf16[512,2048]{1,0:T(8,128)(2,1)} %param.10) | copy-start | bytes 6291460
  6.5 83.7 %all-gather.3.cloned.1.call-start = ((), (), s32[]{:S(2)}) async-start(), calls=%async_computation.1 | async-start | bytes 11141120 | tf_op jit(solution)/shard_map/all_gather | solution.py:59
  90.3 143.8 %collective-permute-start.3 = (bf16[16,256,1280]{2,1,0:T(8,128)(2,1)}, bf16[16,256,1280]{2,1,0:T(8,128)(2,1)}, u32[]{:S(2)}, u32[]{:S(2)}) collective-permute-start(bf16[16,256,1280]{2,1,0:T(8,128)(2,1)} %bitcast.108), channel_id=1, source_target_pairs={{0,4},{4,0},{1,5},{5,1},{2,6},{6,2},{3,7},{7,3},{8,12},{12,8},{9,1... | collective-permute-start | bytes 31457288 | tf_op jit(solution)/shard_map/ppermute | solution.py:60
  95.0 7.1 %copy-start.28 = (s32[512]{0:T(512)S(1)}, s32[512]{0:T(512)}, u32[]{:S(2)}) copy-start(s32[512]{0:T(512)} %param.12) | copy-start | bytes 6148
  95.0 43.7 %all-to-all-start = ((bf16[32,24,2048]{2,1,0:T(8,128)(2,1)}), bf16[32,24,2048]{2,1,0:T(8,128)(2,1)}, u32[]{:S(2)}, u32[]{:S(2)}) async-start(bf16[32,24,2048]{2,1,0:T(8,128)(2,1)} %broadcast_select_fusion), calls=%async_computation | async-start | bytes 6291456 | tf_op jit(solution)/shard_map/all_to_all | solution.py:89
  143.5 6.7 %collective-permute-start.2 = (f32[512]{0:T(512)S(1)}, f32[512]{0:T(512)S(1)}, u32[]{:S(2)}, u32[]{:S(2)}) collective-permute-start(f32[512]{0:T(512)S(1)} %get-tuple-element.67), channel_id=1, source_target_pairs={{0,3},{1,0},{2,1},{3,2},{4,7},{5,4},{6,5},{7,6},{8,11},{9,8},{10,9... | collective-permute-start | bytes 6152 | tf_op jit(solution)/shard_map/ppermute | solution.py:108
  145.9 5.4 %collective-permute-start.1 = (f32[512]{0:T(512)S(1)}, f32[512]{0:T(512)S(1)}, u32[]{:S(2)}, u32[]{:S(2)}) collective-permute-start(f32[512]{0:T(512)S(1)} %get-tuple-element.67), channel_id=1, source_target_pairs={{0,2},{1,3},{2,0},{3,1},{4,6},{5,7},{6,4},{7,5},{8,10},{9,11},{10,... | collective-permute-start | bytes 6152 | tf_op jit(solution)/shard_map/ppermute | solution.py:108
  146.5 5.1 %collective-permute-start = (f32[512]{0:T(512)S(1)}, f32[512]{0:T(512)S(1)}, u32[]{:S(2)}, u32[]{:S(2)}) collective-permute-start(f32[512]{0:T(512)S(1)} %get-tuple-element.67), channel_id=1, source_target_pairs={{0,1},{1,2},{2,3},{3,0},{4,5},{5,6},{6,7},{7,4},{8,9},{9,10},{10,1... | collective-permute-start | bytes 6152 | tf_op jit(solution)/shard_map/ppermute | solution.py:108
  147.1 7.0 %copy-start.29 = (f32[8192]{0:T(1024)S(1)}, f32[8192]{0:T(1024)}, u32[]{:S(2)}) copy-start(f32[8192]{0:T(1024)} %param.13) | copy-start | bytes 98308
  148.7 48.3 %collective-permute-start.5 = (bf16[256,2048]{1,0:T(8,128)(2,1)}, bf16[256,2048]{1,0:T(8,128)(2,1)}, u32[]{:S(2)}, u32[]{:S(2)}) collective-permute-start(bf16[256,2048]{1,0:T(8,128)(2,1)} %get-tuple-element.54), channel_id=1, source_target_pairs={{0,1},{1,2},{2,3},{3,0},{4,5},{5,6},{6,7},{7,4},{8,9},{9,10},{10,1... | collective-permute-start | bytes 3145736 | tf_op jit(solution)/shard_map/ppermute | solution.py:122
  150.2 24.1 %collective-permute-start.7 = (bf16[256,2048]{1,0:T(8,128)(2,1)}, bf16[256,2048]{1,0:T(8,128)(2,1)S(1)}, u32[]{:S(2)}, u32[]{:S(2)}) collective-permute-start(bf16[256,2048]{1,0:T(8,128)(2,1)} %get-tuple-element.54), channel_id=1, source_target_pairs={{0,3},{1,0},{2,1},{3,2},{4,7},{5,4},{6,5},{7,6},{8,11},{9,8},{10,9... | collective-permute-start | bytes 3145736 | tf_op jit(solution)/shard_map/ppermute | solution.py:120
  151.4 45.4 %collective-permute-start.4 = (bf16[256,2048]{1,0:T(8,128)(2,1)}, bf16[256,2048]{1,0:T(8,128)(2,1)}, u32[]{:S(2)}, u32[]{:S(2)}) collective-permute-start(bf16[256,2048]{1,0:T(8,128)(2,1)} %get-tuple-element.53), channel_id=1, source_target_pairs={{0,1},{1,2},{2,3},{3,0},{4,5},{5,6},{6,7},{7,4},{8,9},{9,10},{10,1... | collective-permute-start | bytes 3145736 | tf_op jit(solution)/shard_map/ppermute | solution.py:119
  151.7 45.4 %collective-permute-start.6 = (bf16[256,2048]{1,0:T(8,128)(2,1)}, bf16[256,2048]{1,0:T(8,128)(2,1)}, u32[]{:S(2)}, u32[]{:S(2)}) collective-permute-start(bf16[256,2048]{1,0:T(8,128)(2,1)} %get-tuple-element.53), channel_id=1, source_target_pairs={{0,3},{1,0},{2,1},{3,2},{4,7},{5,4},{6,5},{7,6},{8,11},{9,8},{10,9... | collective-permute-start | bytes 3145736 | tf_op jit(solution)/shard_map/ppermute | solution.py:121
  174.3 44.8 %collective-permute-start.9 = (bf16[256,2048]{1,0:T(8,128)(2,1)S(1)}, bf16[256,2048]{1,0:T(8,128)(2,1)S(1)}, u32[]{:S(2)}, u32[]{:S(2)}) collective-permute-start(bf16[256,2048]{1,0:T(8,128)(2,1)S(1)} %collective-permute-done.7), channel_id=1, source_target_pairs={{0,3},{1,0},{2,1},{3,2},{4,7},{5,4},{6,5},{7,6},{8,11},{9,8},{10,9... | collective-permute-start | bytes 3145736 | tf_op jit(solution)/shard_map/ppermute | solution.py:126
  196.8 24.6 %collective-permute-start.8 = (bf16[256,2048]{1,0:T(8,128)(2,1)}, bf16[256,2048]{1,0:T(8,128)(2,1)S(1)}, u32[]{:S(2)}, u32[]{:S(2)}) collective-permute-start(bf16[256,2048]{1,0:T(8,128)(2,1)} %collective-permute-done.4), channel_id=1, source_target_pairs={{0,1},{1,2},{2,3},{3,0},{4,5},{5,6},{6,7},{7,4},{8,9},{9,10},{10,1... | collective-permute-start | bytes 3145736 | tf_op jit(solution)/shard_map/ppermute | solution.py:125
  222.1 1.0 copy-start.12
  222.1 1.0 copy-start.13
  222.2 1.1 copy-start.14
  222.2 1.2 copy-start.15
  222.2 1.2 copy-start.16
  222.2 1.3 copy-start.17
  222.2 1.4 copy-start.18
  222.2 1.4 copy-start.19
  223.6 3.5 %copy-start.20 = (bf16[512,256]{1,0:T(8,128)(2,1)S(1)}, bf16[512,256]{1,0:T(8,128)(2,1)}, u32[]{:S(2)}) copy-start(bf16[512,256]{1,0:T(8,128)(2,1)} %get-tuple-element.71) | copy-start | bytes 786436
  223.7 3.5 %copy-start.21 = (bf16[512,256]{1,0:T(8,128)(2,1)S(1)}, bf16[512,256]{1,0:T(8,128)(2,1)}, u32[]{:S(2)}) copy-start(bf16[512,256]{1,0:T(8,128)(2,1)} %get-tuple-element.72) | copy-start | bytes 786436
  223.7 3.5 %copy-start.22 = (bf16[512,256]{1,0:T(8,128)(2,1)S(1)}, bf16[512,256]{1,0:T(8,128)(2,1)}, u32[]{:S(2)}) copy-start(bf16[512,256]{1,0:T(8,128)(2,1)} %get-tuple-element.73) | copy-start | bytes 786436
  223.7 3.5 %copy-start.23 = (bf16[512,256]{1,0:T(8,128)(2,1)S(1)}, bf16[512,256]{1,0:T(8,128)(2,1)}, u32[]{:S(2)}) copy-start(bf16[512,256]{1,0:T(8,128)(2,1)} %get-tuple-element.74) | copy-start | bytes 786436
  223.7 3.5 %copy-start.24 = (bf16[512,256]{1,0:T(8,128)(2,1)S(1)}, bf16[512,256]{1,0:T(8,128)(2,1)}, u32[]{:S(2)}) copy-start(bf16[512,256]{1,0:T(8,128)(2,1)} %get-tuple-element.75) | copy-start | bytes 786436
  223.7 3.5 %copy-start.25 = (bf16[512,256]{1,0:T(8,128)(2,1)S(1)}, bf16[512,256]{1,0:T(8,128)(2,1)}, u32[]{:S(2)}) copy-start(bf16[512,256]{1,0:T(8,128)(2,1)} %get-tuple-element.76) | copy-start | bytes 786436
  223.7 3.5 %copy-start.26 = (bf16[512,256]{1,0:T(8,128)(2,1)S(1)}, bf16[512,256]{1,0:T(8,128)(2,1)}, u32[]{:S(2)}) copy-start(bf16[512,256]{1,0:T(8,128)(2,1)} %get-tuple-element.77) | copy-start | bytes 786436
  223.7 3.5 %copy-start.27 = (bf16[512,256]{1,0:T(8,128)(2,1)S(1)}, bf16[512,256]{1,0:T(8,128)(2,1)}, u32[]{:S(2)}) copy-start(bf16[512,256]{1,0:T(8,128)(2,1)} %get-tuple-element.78) | copy-start | bytes 786436
  223.7 7.2 %slice-start = ((s8[10485760]{0:T(1024)(128)(4,1)}), s8[4194304]{0:T(1024)(128)(4,1)S(1)}, s32[]{:S(2)}) async-start(s8[10485760]{0:T(1024)(128)(4,1)} %bitcast.111), calls=%async_computation.2 | async-start | bytes 8388608
  223.7 7.2 %slice-start.1 = ((s8[10485760]{0:T(1024)(128)(4,1)}), s8[4194304]{0:T(1024)(128)(4,1)S(1)}, s32[]{:S(2)}) async-start(s8[10485760]{0:T(1024)(128)(4,1)} %bitcast.111), calls=%async_computation.3 | async-start | bytes 8388608
  227.2 3.7 %copy-start.4 = (bf16[512,256]{1,0:T(8,128)(2,1)S(1)}, bf16[512,256]{1,0:T(8,128)(2,1)}, u32[]{:S(2)}) copy-start(bf16[512,256]{1,0:T(8,128)(2,1)} %get-tuple-element.29) | copy-start | bytes 786436
  227.2 3.7 %copy-start.5 = (bf16[512,256]{1,0:T(8,128)(2,1)S(1)}, bf16[512,256]{1,0:T(8,128)(2,1)}, u32[]{:S(2)}) copy-start(bf16[512,256]{1,0:T(8,128)(2,1)} %get-tuple-element.30) | copy-start | bytes 786436
  227.2 3.7 %copy-start.6 = (bf16[512,256]{1,0:T(8,128)(2,1)S(1)}, bf16[512,256]{1,0:T(8,128)(2,1)}, u32[]{:S(2)}) copy-start(bf16[512,256]{1,0:T(8,128)(2,1)} %get-tuple-element.31) | copy-start | bytes 786436
  227.3 3.7 %copy-start.7 = (bf16[512,256]{1,0:T(8,128)(2,1)S(1)}, bf16[512,256]{1,0:T(8,128)(2,1)}, u32[]{:S(2)}) copy-start(bf16[512,256]{1,0:T(8,128)(2,1)} %get-tuple-element.32) | copy-start | bytes 786436
  227.3 3.7 %copy-start.8 = (bf16[512,256]{1,0:T(8,128)(2,1)S(1)}, bf16[512,256]{1,0:T(8,128)(2,1)}, u32[]{:S(2)}) copy-start(bf16[512,256]{1,0:T(8,128)(2,1)} %get-tuple-element.33) | copy-start | bytes 786436
  227.3 3.7 %copy-start.9 = (bf16[512,256]{1,0:T(8,128)(2,1)S(1)}, bf16[512,256]{1,0:T(8,128)(2,1)}, u32[]{:S(2)}) copy-start(bf16[512,256]{1,0:T(8,128)(2,1)} %get-tuple-element.34) | copy-start | bytes 786436
  227.3 3.7 %copy-start.10 = (bf16[512,256]{1,0:T(8,128)(2,1)S(1)}, bf16[512,256]{1,0:T(8,128)(2,1)}, u32[]{:S(2)}) copy-start(bf16[512,256]{1,0:T(8,128)(2,1)} %get-tuple-element.35) | copy-start | bytes 786436
  227.3 3.7 %copy-start.11 = (bf16[512,256]{1,0:T(8,128)(2,1)S(1)}, bf16[512,256]{1,0:T(8,128)(2,1)}, u32[]{:S(2)}) copy-start(bf16[512,256]{1,0:T(8,128)(2,1)} %get-tuple-element.36) | copy-start | bytes 786436
  227.3 3.7 %slice-start.2 = ((s8[10485760]{0:T(1024)(128)(4,1)}), s8[2097152]{0:T(1024)(128)(4,1)S(1)}, s32[]{:S(2)}) async-start(s8[10485760]{0:T(1024)(128)(4,1)} %bitcast.111), calls=%async_computation.4 | async-start | bytes 4194304
  244.2 3.4 %copy-start.30 = (f32[1024]{0:T(1024)S(1)}, f32[1024]{0:T(1024)}, u32[]{:S(2)}) copy-start(f32[1024]{0:T(1024)} %param.17) | copy-start | bytes 12292
  248.6 0.7 copy-start.31
  248.6 2.0 copy-start.2
  248.6 2.0 copy-start.3
  253.6 1.8 copy-start.32
  255.3 4.0 %copy-start.1 = (bf16[512,2048]{1,0:T(8,128)(2,1)S(1)}, bf16[512,2048]{1,0:T(8,128)(2,1)}, u32[]{:S(2)}) copy-start(bf16[512,2048]{1,0:T(8,128)(2,1)} %param.10) | copy-start | bytes 6291460
Sparse Core Ops, SparseCore 0:
  9.5 80.7 all-gather.2
